TPU v7x, 128 devices: a whole 4x4x4 slice. The times are simulated.
128 devices in a mesh: chan: 8 (over y_hi, x), tm: 16 (over z, y_lo, core).
Axes of the slice: x: 4, y: 4 (y_hi: 2, y_lo: 2; y = y_hi * 2 + y_lo), z: 4, core: 2. Of those that a mesh axis runs over, the one named last changes fastest.
Arguments:
- traces: bfloat16 [128, 1024, 2048], P('tm', 'chan'), may hold values from -6 to 6
- live: int32 [1024], P('chan'), may hold values 0 or 1
Outputs:
- correlations: bfloat16 [1024, 128, 2048], P(('chan', 'tm'))
Inputs may be any that keep to these rules, and one draw needn't show every extreme that they name: `live`: 1 marks a usable channel, 0 a dead one.
All inputs are finite; a program needn't handle non-finite values. No bound on the sum of `live` on one device may be relied on, other than what follows from the above.
Results may differ from a plain program's by a relative error of at most 0.0076.
Values may be sent and summed in bfloat16 or wider, within the bound.
No kernel may reach another device: no remote copies, remote signals or barrier semaphores. Data moves between devices by JAX's collectives and lax.ppermute only.
A program may use at most 128 MiB of HBM per device.

v0:
```python
import math

import jax
import jax.numpy as jnp
import numpy as np
from jax import lax
from jax.experimental import pallas as pl
from jax.experimental.pallas import tpu as pltpu
from jax.sharding import PartitionSpec as P

SMOOTH = 4


def from_behind(block, axis, distance):
    devices = range(lax.axis_size(axis))
    route = [(i - distance, i) for i in devices if i - distance in devices]
    return lax.ppermute(block, axis, route)


def column_bins(count, group_width):
    index = np.arange(count, dtype=np.int64)
    group = index // (2 * group_width)
    within = index % group_width
    is_imag = index // group_width % 2
    return (group * group_width + within, is_imag)


def forward_table(samples, bins, group_width):
    freq, is_imag = column_bins(2 * bins, group_width)
    moments = np.arange(samples, dtype=np.int64)[:, None]
    phase = (moments * freq[None, :] % samples).astype(np.float32) * np.float32(2.0 * math.pi / samples)
    phase = phase.astype(np.float64)
    table = np.where(is_imag[None, :] == 1, -np.sin(phase), np.cos(phase)).astype(np.float32)
    return jnp.asarray(table.astype(jnp.bfloat16))


def inverse_table(samples, bins, group_width, segments):
    freq, is_imag = column_bins(2 * bins, group_width)
    lag = np.arange(samples, dtype=np.int64) - samples // 2
    phase = np.mod(freq[:, None] * lag[None, :], samples).astype(np.float32) * np.float32(
        2.0 * math.pi / samples
    )
    phase = phase.astype(np.float64)
    weight = np.where(freq == 0, 1.0, 2.0).astype(np.float32) / np.float32(math.sqrt(samples * segments))
    wave = np.where(is_imag[:, None] == 1, -np.sin(phase), np.cos(phase)).astype(np.float32)
    return jnp.asarray((weight[:, None] * wave).astype(np.float32).astype(jnp.bfloat16))


def whiten_cols(spectra, groups):
    bins = spectra.shape[0] // 2
    width = bins // groups
    rest = spectra.shape[1:]
    split = spectra.reshape((groups, 2, width) + rest)
    real_part = split[:, 0].reshape((bins,) + rest)
    imag_part = split[:, 1].reshape((bins,) + rest)
    amplitude = jnp.sqrt(real_part * real_part + imag_part * imag_part)
    padded = jnp.pad(amplitude, [(SMOOTH, SMOOTH)] + [(0, 0)] * len(rest))
    smooth = sum((padded[i : i + bins] for i in range(2 * SMOOTH + 1))) / (2 * SMOOTH + 1)
    water = 0.8 * jnp.mean(amplitude, axis=0, keepdims=True) + 1e-06
    level = jnp.maximum(smooth, water).reshape((groups, 1, width) + rest)
    return (split / level).reshape(spectra.shape)


def cross_kernel(own_ref, next_ref, wrap_ref, out_ref):
    block = own_ref.shape[2]
    row = lax.broadcasted_iota(jnp.int32, (block, block), 0)
    col = lax.broadcasted_iota(jnp.int32, (block, block), 1)
    flip = (row + col == block - 1).astype(jnp.bfloat16)

    def reverse_rows(x):
        return jnp.dot(flip, x, preferred_element_type=jnp.float32).astype(jnp.bfloat16)

    for f in range(own_ref.shape[1]):
        own_real = own_ref[0, f]
        own_imag = own_ref[1, f]
        own_both = jnp.concatenate([own_real, own_imag], axis=1)
        lhs = jnp.concatenate(
            [own_both, jnp.concatenate([own_imag, -own_real], axis=1)], axis=0
        )
        next_both = jnp.concatenate(
            [next_ref[0, f] + wrap_ref[0, f], next_ref[1, f] + wrap_ref[1, f]], axis=1
        )
        rhs = jnp.concatenate([reverse_rows(next_both), reverse_rows(own_both)], axis=0)
        both = lax.dot_general(
            lhs, rhs, (((1,), (1,)), ((), ())), preferred_element_type=jnp.float32
        )
        for part in range(2):
            rows = both[part * block : (part + 1) * block]
            sheared = pltpu.roll(rows, 1, 1, stride=1, stride_axis=0)[:, block:]
            ordered = jnp.dot(
                sheared.astype(jnp.bfloat16), flip, preferred_element_type=jnp.float32
            )
            out_ref[:, part, f] = ordered.reshape(out_ref.shape[0], -1, block).astype(out_ref.dtype)


def cross(own_t, next_t, wrap_t, parts, interpret=False):
    two, width, block, segs = own_t.shape
    step = min(width, 8)
    spec = pl.BlockSpec((two, step, block, segs), lambda i: (0, i, 0, 0))
    return pl.pallas_call(
        cross_kernel,
        grid=(width // step,),
        in_specs=[spec, spec, spec],
        out_specs=pl.BlockSpec(
            (parts, two, step, block // parts, block), lambda i: (0, 0, i, 0, 0)
        ),
        out_shape=jax.ShapeDtypeStruct((parts, two, width, block // parts, block), jnp.bfloat16),
        interpret=interpret,
    )(own_t, next_t, wrap_t)


CHUNKS = 2
ROW = 4


def body(traces, live):
    seg_dev, block, samples = traces.shape
    bins = samples // 2
    groups = lax.axis_size("tm")
    group_width = bins // groups
    width = group_width // CHUNKS
    segments = seg_dev * groups
    table = forward_table(samples, bins, group_width)
    inverse = inverse_table(samples, bins, group_width, segments).reshape(
        groups, 2, CHUNKS, width, samples
    )
    spectra = jnp.einsum("jat,tc->cja", traces, table, preferred_element_type=jnp.float32)
    flags = live.astype(jnp.float32)
    white = (whiten_cols(spectra, groups) * flags).astype(jnp.bfloat16)
    white = white.reshape(groups, 2, CHUNKS, width, seg_dev, block)
    blocks = lax.axis_size("chan")
    inner_route = [(i + 1, i) for i in range(blocks - 1) if (i + 1) % ROW != 0]
    wrap_route = [
        ((i + 1) * groups + m, i * groups + (m ^ 2))
        for i in range(blocks - 1)
        if (i + 1) % ROW == 0
        for m in range(groups)
    ]
    swapped = lax.axis_index("chan") < ROW

    def swap_pairs(x):
        split = x.reshape((groups // 4, 2, 2) + x.shape[1:])
        return jnp.where(swapped, split[:, ::-1], split).reshape(x.shape)

    lagged = None
    for chunk in range(CHUNKS):
        piece = swap_pairs(white[:, :, chunk]).reshape(groups * 2 * width, seg_dev, block)
        own = lax.all_to_all(piece, "tm", split_axis=0, concat_axis=1, tiled=True)
        own_t = jnp.swapaxes(own, 1, 2).reshape(2, width, block, segments)
        next_t = lax.ppermute(own_t, "chan", inner_route)
        wrap_t = lax.ppermute(own_t, ("chan", "tm"), wrap_route)
        stack = cross(own_t, next_t, wrap_t, groups)
        gathered = lax.all_to_all(stack, "tm", split_axis=0, concat_axis=0, tiled=True)
        gathered = swap_pairs(gathered).reshape(groups * 2 * width, block // groups, block)
        rows = inverse[:, :, chunk].reshape(groups * 2 * width, samples)
        part = jnp.einsum("hak,hl->akl", gathered, rows, preferred_element_type=jnp.float32)
        lagged = part if lagged is None else lagged + part
    return lagged.astype(jnp.bfloat16)


def solution(mesh):
    in_specs = (P("tm", "chan", None), P("chan"))
    out_specs = P(("chan", "tm"), None, None)
    return jax.shard_map(body, mesh=mesh, in_specs=in_specs, out_specs=out_specs, check_vma=False)
```

profile of v0, /device:TPU:6, one launch (start us, length us, event | category | flops | bytes accessed | tf_op | source)
XLA Modules:
  0.0 254.5 jit_solution(5861690194624766719)
XLA Ops:
  0.0 12.5 %fusion.12 = f32[2048,8,128]{2,0,1:T(8,128)S(1)} fusion(bf16[2048,2048,1]{0,1,2:T(8,128)(2,1)} %constant.36, bf16[8,128,2048]{2,1,0:T(8,128)(2,1)} %param.4), kind=kOutput, calls=%fused_computation.26 | convolution fusion | flops 8589934592 | bytes 20971520 | tf_op jit(solution)/shard_map/jat,tc->cja/dot_general | solution.py:127
  12.6 3.5 %fusion.9 = (f32[8,128]{1,0:T(8,128)S(1)}, f32[16,1,64,8,128]{4,2,1,0,3:T(8,128)}) fusion(f32[16,2,64,8,128]{4,2,1,0,3:T(8,128)S(1)} %bitcast.43), kind=kLoop, calls=%fused_computation.24 | loop fusion | flops 4193280 | bytes 12587008 | tf_op jit(solution)/shard_map/reduce_sum | solution.py:59
  16.1 17.0 %multiply_maximum_fusion = f32[1024,8,128]{2,0,1:T(8,128)S(1)} fusion(f32[1024,8,128]{2,0,1:T(8,128)} %bitcast.46, f32[8,128]{1,0:T(8,128)S(1)} %multiply_add_fusion), kind=kLoop, calls=%fused_computation.8 | loop fusion | flops 10485760 | bytes 8392704 | tf_op jit(solution)/shard_map/max | solution.py:60
  41.8 6.4 %all-to-all-start.2 = ((bf16[1024,8,128]{2,1,0:T(8,128)(2,1)}), bf16[1024,8,128]{2,1,0:T(8,128)(2,1)S(1)}, u32[]{:S(2)}, u32[]{:S(2)}) async-start(bf16[1024,8,128]{2,1,0:T(8,128)(2,1)} %bitcast.52), calls=%async_computation.2 | async-start | bytes 4194304 | tf_op jit(solution)/shard_map/all_to_all | solution.py:148
  48.2 4.9 %copy.17 = bf16[16,2,1,32,8,128]{5,4,3,1,0,2:T(8,128)(2,1)S(1)} copy(bf16[16,2,1,32,8,128]{5,3,2,1,0,4:T(8,128)(2,1)} %get-tuple-element.8) | data formatting | bytes 4194304 | tf_op jit(solution)/shard_map/slice | solution.py:147
  55.0 21.0 %all-to-all-done.2 = bf16[1024,8,128]{2,1,0:T(8,128)(2,1)S(1)} async-done(((bf16[1024,8,128]{2,1,0:T(8,128)(2,1)}), bf16[1024,8,128]{2,1,0:T(8,128)(2,1)S(1)}, u32[]{:S(2)}, u32[]{:S(2)}) %all-to-all-start.2) | async-done | bytes 2097184 | tf_op jit(solution)/shard_map/all_to_all | solution.py:148
  77.4 3.7 %all-to-all-start = ((bf16[1024,8,128]{2,1,0:T(8,128)(2,1)}), bf16[1024,8,128]{2,1,0:T(8,128)(2,1)S(1)}, u32[]{:S(2)}, u32[]{:S(2)}) async-start(bf16[1024,8,128]{2,1,0:T(8,128)(2,1)} %bitcast.7), calls=%async_computation | async-start | bytes 4194304 | tf_op jit(solution)/shard_map/all_to_all | solution.py:148
  81.1 3.5 %copy.31 = bf16[64,16,8,128]{3,2,1,0:T(8,128)(2,1)} copy(bf16[64,16,8,128]{3,2,0,1:T(8,128)(2,1)} %bitcast.50) | data formatting | bytes 4194304 | tf_op jit(solution)/shard_map/all_to_all | solution.py:148
  84.6 4.1 %copy.23 = bf16[64,128,128]{2,1,0:T(8,128)(2,1)} copy(bf16[64,128,128]{1,2,0:T(8,128)(2,1)} %bitcast.54) | data formatting | bytes 4194304 | tf_op jit(solution)/shard_map/transpose | solution.py:149
  88.7 4.1 %collective-permute-start.2 = (bf16[2,32,128,128]{3,2,1,0:T(8,128)(2,1)}, bf16[2,32,128,128]{3,2,1,0:T(8,128)(2,1)}, u32[]{:S(2)}, u32[]{:S(2)}) collective-permute-start(bf16[2,32,128,128]{3,2,1,0:T(8,128)(2,1)} %bitcast.56), channel_id=1, source_target_pairs={{16,0},{32,16},{48,32},{80,64},{96,80},{112,96},{17,1},{33,17},{49... | collective-permute-start | bytes 6291464 | tf_op jit(solution)/shard_map/ppermute | solution.py:150
  94.1 14.8 %all-to-all-done = bf16[1024,8,128]{2,1,0:T(8,128)(2,1)S(1)} async-done(((bf16[1024,8,128]{2,1,0:T(8,128)(2,1)}), bf16[1024,8,128]{2,1,0:T(8,128)(2,1)S(1)}, u32[]{:S(2)}, u32[]{:S(2)}) %all-to-all-start) | async-done | bytes 2097184 | tf_op jit(solution)/shard_map/all_to_all | solution.py:148
  110.8 4.1 %copy.19 = bf16[64,128,128]{2,1,0:T(8,128)(2,1)} copy(bf16[64,128,128]{1,2,0:T(8,128)(2,1)} %bitcast.55) | data formatting | bytes 4194304 | tf_op jit(solution)/shard_map/transpose | solution.py:149
  114.9 4.1 %collective-permute-start = (bf16[2,32,128,128]{3,2,1,0:T(8,128)(2,1)}, bf16[2,32,128,128]{3,2,1,0:T(8,128)(2,1)}, u32[]{:S(2)}, u32[]{:S(2)}) collective-permute-start(bf16[2,32,128,128]{3,2,1,0:T(8,128)(2,1)} %bitcast.12.own_ref), channel_id=1, source_target_pairs={{16,0},{32,16},{48,32},{80,64},{96,80},{112,96},{17,1},{33,17},{49... | collective-permute-start | bytes 6291464 | tf_op jit(solution)/shard_map/ppermute | solution.py:150
  120.3 17.5 %collective-permute-done.2.next_ref = bf16[2,32,128,128]{3,2,1,0:T(8,128)(2,1)} collective-permute-done((bf16[2,32,128,128]{3,2,1,0:T(8,128)(2,1)}, bf16[2,32,128,128]{3,2,1,0:T(8,128)(2,1)}, u32[]{:S(2)}, u32[]{:S(2)}) %collective-permute-start.2) | collective-permute-done | bytes 2097184 | tf_op jit(solution)/shard_map/ppermute | solution.py:150
  137.8 9.1 %collective-permute-done.3.wrap_ref = bf16[2,32,128,128]{3,2,1,0:T(8,128)(2,1)} collective-permute-done((bf16[2,32,128,128]{3,2,1,0:T(8,128)(2,1)}, bf16[2,32,128,128]{3,2,1,0:T(8,128)(2,1)}, u32[]{:S(2)}, u32[]{:S(2)}) %collective-permute-start.3) | collective-permute-done | bytes 2097184 | tf_op jit(solution)/shard_map/ppermute | solution.py:151
  146.8 17.0 %shard_map.47 = bf16[16,2,32,8,128]{4,3,2,1,0:T(8,128)(2,1)} custom-call(bf16[2,32,128,128]{3,2,1,0:T(8,128)(2,1)} %bitcast.58, bf16[2,32,128,128]{3,2,1,0:T(8,128)(2,1)} %collective-permute-done.2.next_ref, bf16[2,32,128,128]{3,2,1,0:T(8,128)(2,1)} %collective-permute-done.3.wrap_ref), custom_call_target="tpu_custom_call" | custom-call | tf_op jit(solution)/shard_map/pallas_call | solution.py:100
  163.8 4.7 %all-to-all-start.3 = ((bf16[16,2,32,8,128]{4,3,2,1,0:T(8,128)(2,1)}), bf16[16,2,32,8,128]{4,3,2,1,0:T(8,128)(2,1)S(1)}, u32[]{:S(2)}, u32[]{:S(2)}) async-start(bf16[16,2,32,8,128]{4,3,2,1,0:T(8,128)(2,1)} %shard_map.47), calls=%async_computation.3 | async-start | bytes 4194304 | tf_op jit(solution)/shard_map/all_to_all | solution.py:153
  168.5 13.5 %collective-permute-done.next_ref = bf16[2,32,128,128]{3,2,1,0:T(8,128)(2,1)} collective-permute-done((bf16[2,32,128,128]{3,2,1,0:T(8,128)(2,1)}, bf16[2,32,128,128]{3,2,1,0:T(8,128)(2,1)}, u32[]{:S(2)}, u32[]{:S(2)}) %collective-permute-start) | collective-permute-done | bytes 2097184 | tf_op jit(solution)/shard_map/ppermute | solution.py:150
  182.0 8.8 %collective-permute-done.1.wrap_ref = bf16[2,32,128,128]{3,2,1,0:T(8,128)(2,1)} collective-permute-done((bf16[2,32,128,128]{3,2,1,0:T(8,128)(2,1)}, bf16[2,32,128,128]{3,2,1,0:T(8,128)(2,1)}, u32[]{:S(2)}, u32[]{:S(2)}) %collective-permute-start.1) | collective-permute-done | bytes 2097184 | tf_op jit(solution)/shard_map/ppermute | solution.py:151
  190.8 16.9 %shard_map.46 = bf16[16,2,32,8,128]{4,3,2,1,0:T(8,128)(2,1)} custom-call(bf16[2,32,128,128]{3,2,1,0:T(8,128)(2,1)} %bitcast.12.own_ref, bf16[2,32,128,128]{3,2,1,0:T(8,128)(2,1)} %collective-permute-done.next_ref, bf16[2,32,128,128]{3,2,1,0:T(8,128)(2,1)} %collective-permute-done.1.wrap_ref), custom_call_target="tpu_custom_call" | custom-call | tf_op jit(solution)/shard_map/pallas_call | solution.py:100
  207.7 4.6 %all-to-all-start.1 = ((bf16[16,2,32,8,128]{4,3,2,1,0:T(8,128)(2,1)}), bf16[16,2,32,8,128]{4,3,2,1,0:T(8,128)(2,1)}, u32[]{:S(2)}, u32[]{:S(2)}) async-start(bf16[16,2,32,8,128]{4,3,2,1,0:T(8,128)(2,1)} %shard_map.46), calls=%async_computation.1 | async-start | bytes 4194304 | tf_op jit(solution)/shard_map/all_to_all | solution.py:153
  215.4 24.9 %all-to-all-done.1 = bf16[16,2,32,8,128]{4,3,2,1,0:T(8,128)(2,1)} async-done(((bf16[16,2,32,8,128]{4,3,2,1,0:T(8,128)(2,1)}), bf16[16,2,32,8,128]{4,3,2,1,0:T(8,128)(2,1)}, u32[]{:S(2)}, u32[]{:S(2)}) %all-to-all-start.1) | async-done | bytes 2097184 | tf_op jit(solution)/shard_map/all_to_all | solution.py:153
  243.7 4.6 %fusion.7 = f32[8,128,2048]{2,1,0:T(8,128)S(1)} fusion(bf16[1024,2048,1]{1,0,2:T(8,128)(2,1)S(1)} %copy-done.4, bf16[1024,8,128]{2,1,0:T(8,128)(2,1)S(1)} %bitcast.59), kind=kOutput, calls=%fused_computation.20 | convolution fusion | flops 4294967296 | bytes 14680064 | tf_op jit(solution)/shard_map/hak,hl->akl/dot_general | solution.py:156
  248.3 6.2 %add_convert_fusion = bf16[8,128,2048]{2,1,0:T(8,128)(2,1)} fusion(f32[8,128,2048]{2,1,0:T(8,128)S(1)} %fusion.7, bf16[1024,2048,1]{1,0,2:T(8,128)(2,1)S(1)} %copy-done.2, bf16[1024,8,128]{2,1,0:T(8,128)(2,1)S(1)} %bitcast.47), kind=kOutput, calls=%fused_computation.3 | convolution fusion | flops 4299161600 | bytes 18874368 | tf_op jit(solution)/shard_map/hak,hl->akl/dot_general | solution.py:156
  (23 shorter events, 22.8 us)
Async XLA Ops:
  12.6 3.5 %copy-start.3 = (s32[128]{0:T(128)S(1)}, s32[128]{0:T(128)}, u32[]{:S(2)}) copy-start(s32[128]{0:T(128)} %param.5) | copy-start | bytes 1540
  41.8 34.3 %all-to-all-start.2 = ((bf16[1024,8,128]{2,1,0:T(8,128)(2,1)}), bf16[1024,8,128]{2,1,0:T(8,128)(2,1)S(1)}, u32[]{:S(2)}, u32[]{:S(2)}) async-start(bf16[1024,8,128]{2,1,0:T(8,128)(2,1)} %bitcast.52), calls=%async_computation.2 | async-start | bytes 4194304 | tf_op jit(solution)/shard_map/all_to_all | solution.py:148
  76.0 1.3 copy-start.1
  77.4 31.5 %all-to-all-start = ((bf16[1024,8,128]{2,1,0:T(8,128)(2,1)}), bf16[1024,8,128]{2,1,0:T(8,128)(2,1)S(1)}, u32[]{:S(2)}, u32[]{:S(2)}) async-start(bf16[1024,8,128]{2,1,0:T(8,128)(2,1)} %bitcast.7), calls=%async_computation | async-start | bytes 4194304 | tf_op jit(solution)/shard_map/all_to_all | solution.py:148
  88.7 49.1 %collective-permute-start.2 = (bf16[2,32,128,128]{3,2,1,0:T(8,128)(2,1)}, bf16[2,32,128,128]{3,2,1,0:T(8,128)(2,1)}, u32[]{:S(2)}, u32[]{:S(2)}) collective-permute-start(bf16[2,32,128,128]{3,2,1,0:T(8,128)(2,1)} %bitcast.56), channel_id=1, source_target_pairs={{16,0},{32,16},{48,32},{80,64},{96,80},{112,96},{17,1},{33,17},{49... | collective-permute-start | bytes 6291464 | tf_op jit(solution)/shard_map/ppermute | solution.py:150
  92.8 54.0 %collective-permute-start.3 = (bf16[2,32,128,128]{3,2,1,0:T(8,128)(2,1)}, bf16[2,32,128,128]{3,2,1,0:T(8,128)(2,1)}, u32[]{:S(2)}, u32[]{:S(2)}) collective-permute-start(bf16[2,32,128,128]{3,2,1,0:T(8,128)(2,1)} %bitcast.57), channel_id=1, source_target_pairs={{64,50},{65,51},{66,48},{67,49},{68,54},{69,55},{70,52},{71,53},{7... | collective-permute-start | bytes 6291464 | tf_op jit(solution)/shard_map/ppermute | solution.py:151
  114.9 67.1 %collective-permute-start = (bf16[2,32,128,128]{3,2,1,0:T(8,128)(2,1)}, bf16[2,32,128,128]{3,2,1,0:T(8,128)(2,1)}, u32[]{:S(2)}, u32[]{:S(2)}) collective-permute-start(bf16[2,32,128,128]{3,2,1,0:T(8,128)(2,1)} %bitcast.12.own_ref), channel_id=1, source_target_pairs={{16,0},{32,16},{48,32},{80,64},{96,80},{112,96},{17,1},{33,17},{49... | collective-permute-start | bytes 6291464 | tf_op jit(solution)/shard_map/ppermute | solution.py:150
  119.0 71.8 %collective-permute-start.1 = (bf16[2,32,128,128]{3,2,1,0:T(8,128)(2,1)}, bf16[2,32,128,128]{3,2,1,0:T(8,128)(2,1)}, u32[]{:S(2)}, u32[]{:S(2)}) collective-permute-start(bf16[2,32,128,128]{3,2,1,0:T(8,128)(2,1)} %bitcast.12.own_ref), channel_id=1, source_target_pairs={{64,50},{65,51},{66,48},{67,49},{68,54},{69,55},{70,52},{71,53},{7... | collective-permute-start | bytes 6291464 | tf_op jit(solution)/shard_map/ppermute | solution.py:151
  163.8 43.9 %all-to-all-start.3 = ((bf16[16,2,32,8,128]{4,3,2,1,0:T(8,128)(2,1)}), bf16[16,2,32,8,128]{4,3,2,1,0:T(8,128)(2,1)S(1)}, u32[]{:S(2)}, u32[]{:S(2)}) async-start(bf16[16,2,32,8,128]{4,3,2,1,0:T(8,128)(2,1)} %shard_map.47), calls=%async_computation.3 | async-start | bytes 4194304 | tf_op jit(solution)/shard_map/all_to_all | solution.py:153
  207.7 4.6 %copy-start = (bf16[16,2,32,8,128]{4,3,2,1,0:T(8,128)(2,1)}, bf16[16,2,32,8,128]{4,3,2,1,0:T(8,128)(2,1)S(1)}, u32[]{:S(2)}) copy-start(bf16[16,2,32,8,128]{4,3,2,1,0:T(8,128)(2,1)S(1)} %all-to-all-done.3) | copy-start | bytes 6291460
  207.7 32.5 %all-to-all-start.1 = ((bf16[16,2,32,8,128]{4,3,2,1,0:T(8,128)(2,1)}), bf16[16,2,32,8,128]{4,3,2,1,0:T(8,128)(2,1)}, u32[]{:S(2)}, u32[]{:S(2)}) async-start(bf16[16,2,32,8,128]{4,3,2,1,0:T(8,128)(2,1)} %shard_map.46), calls=%async_computation.1 | async-start | bytes 4194304 | tf_op jit(solution)/shard_map/all_to_all | solution.py:153
  240.3 3.4 %copy-start.4 = (bf16[1024,2048,1]{1,0,2:T(8,128)(2,1)S(1)}, bf16[1024,2048,1]{1,0,2:T(8,128)(2,1)}, u32[]{:S(2)}) copy-start(bf16[1024,2048,1]{1,0,2:T(8,128)(2,1)} %constant.37) | copy-start | bytes 12582916
  243.7 4.6 %copy-start.2 = (bf16[1024,2048,1]{1,0,2:T(8,128)(2,1)S(1)}, bf16[1024,2048,1]{1,0,2:T(8,128)(2,1)}, u32[]{:S(2)}) copy-start(bf16[1024,2048,1]{1,0,2:T(8,128)(2,1)} %constant.38) | copy-start | bytes 12582916
where the time goes:
time: 255 us
  waiting for transfers between devices  110 us (43%)
  Pallas kernels  33.9 us (13%)
  other arithmetic  31.7 us (12%)
  starting transfers between devices  30.3 us (12%)
  local copies, waits for them, and re-layouts  25.7 us (10%)
  matrix products  23.3 us (9%)
    all_to_all x2, waiting for transfers between devices, body(): own = lax.all_to_all(piece, 'tm', split_axis=0, concat_axis=1, tiled=True)  35.8 us
    pallas_call x2, Pallas kernels, cross(): pl.pallas_call(cross_kernel, grid=(width // step,), in_specs=[spec, spec,...  33.9 us
    ppermute x2, waiting for transfers between devices, body(): next_t = lax.ppermute(own_t, 'chan', inner_route)  31 us
    all_to_all x2, waiting for transfers between devices, body(): lax.all_to_all(stack, 'tm', split_axis=0, concat_axis=0, tiled=True)  24.9 us
    ppermute x2, waiting for transfers between devices, body(): wrap_t = lax.ppermute(own_t, ('chan', 'tm'), wrap_route)  17.9 us
    max x1, other arithmetic, whiten_cols(): level = jnp.maximum(smooth, water).reshape((groups, 1, width) + rest)  17 us
    dot_general x1, matrix products, body(): jnp.einsum('jat,tc->cja', traces, table, preferred_element_type=jnp.float32)  12.5 us
    dot_general x2, matrix products, body(): jnp.einsum('hak,hl->akl', gathered, rows, preferred_element_type=jnp.floa...  10.8 us
  transfers between devices with their start and end apart: 8, of which 7 were waited for; matrix products, arithmetic and copies ran while one was open for 9% of the time, Pallas kernels for 13%

commit v1 on v0

--- a/solution.py
+++ b/solution.py
@@ -151,8 +151,8 @@
         wrap_t = lax.ppermute(own_t, ("chan", "tm"), wrap_route)
         stack = cross(own_t, next_t, wrap_t, groups)
         gathered = lax.all_to_all(stack, "tm", split_axis=0, concat_axis=0, tiled=True)
-        gathered = swap_pairs(gathered).reshape(groups * 2 * width, block // groups, block)
-        rows = inverse[:, :, chunk].reshape(groups * 2 * width, samples)
+        gathered = gathered.reshape(groups * 2 * width, block // groups, block)
+        rows = swap_pairs(inverse[:, :, chunk]).reshape(groups * 2 * width, samples)
         part = jnp.einsum("hak,hl->akl", gathered, rows, preferred_element_type=jnp.float32)
         lagged = part if lagged is None else lagged + part
     return lagged.astype(jnp.bfloat16)

time: 255 us -> 250 us (0.980)
  waiting for transfers between devices: 110 us -> 97.5 us
  matrix products: 23.3 us -> 30.7 us
    all_to_all x2, waiting for transfers between devices: 24.9 us -> 12.2 us  [body(): lax.all_to_all(stack, 'tm', split_axis=0, concat_axis=0, tiled=True)]
    slice x3 -> x1, local copies, waits for them, and re-layouts: 10.4 us -> 2.19 us  [body(): white[:, :, chunk]]
    another operation x0 -> x2, local copies, waits for them, and re-layouts: none -> 8.22 us  [swap_pairs(): split = x.reshape((groups // 4, 2, 2) + x.shape[1:])]
    dot_general x2, matrix products: 10.8 us -> 18.1 us  [body(): jnp.einsum('hak,hl->akl', gathered, rows, preferred_element_type=jnp.floa...]
  transfers between devices with their start and end apart: 8 -> 8, of which waited for: 7 -> 7; matrix products, arithmetic and copies ran while one was open for 9% -> 13% of each run, Pallas kernels for 13% -> 14%
where the time goes in v1:
time: 250 us; the launch traced here: 249 us
  waiting for transfers between devices  97.5 us (39%)
  Pallas kernels  33.9 us (14%)
  matrix products  30.7 us (12%)
  other arithmetic  30.4 us (12%)
  starting transfers between devices  30.2 us (12%)
  local copies, waits for them, and re-layouts  26.4 us (11%)
    all_to_all x2, waiting for transfers between devices, body(): own = lax.all_to_all(piece, 'tm', split_axis=0, concat_axis=1, tiled=True)  35.8 us
    pallas_call x2, Pallas kernels, cross(): pl.pallas_call(cross_kernel, grid=(width // step,), in_specs=[spec, spec,...  33.9 us
    ppermute x2, waiting for transfers between devices, body(): next_t = lax.ppermute(own_t, 'chan', inner_route)  31.6 us
    dot_general x2, matrix products, body(): jnp.einsum('hak,hl->akl', gathered, rows, preferred_element_type=jnp.floa...  18.1 us
    ppermute x2, waiting for transfers between devices, body(): wrap_t = lax.ppermute(own_t, ('chan', 'tm'), wrap_route)  17.9 us
    max x1, other arithmetic, whiten_cols(): level = jnp.maximum(smooth, water).reshape((groups, 1, width) + rest)  16.6 us
    dot_general x1, matrix products, body(): jnp.einsum('jat,tc->cja', traces, table, preferred_element_type=jnp.float32)  12.5 us
    all_to_all x2, waiting for transfers between devices, body(): lax.all_to_all(stack, 'tm', split_axis=0, concat_axis=0, tiled=True)  12.2 us
  transfers between devices with their start and end apart: 8, of which 7 were waited for; matrix products, arithmetic and copies ran while one was open for 13% of the time, Pallas kernels for 14%

profile of v1, /device:TPU:6, one launch (start us, length us, event | category | flops | bytes accessed | tf_op | source)
XLA Modules:
  0.0 249.3 jit_solution(16370923228108165988)
XLA Ops:
  0.0 12.5 %fusion.12 = f32[2048,8,128]{2,0,1:T(8,128)S(1)} fusion(bf16[2048,2048,1]{0,1,2:T(8,128)(2,1)} %constant.38, bf16[8,128,2048]{2,1,0:T(8,128)(2,1)} %param.4), kind=kOutput, calls=%fused_computation.26 | convolution fusion | flops 8589934592 | bytes 20971520 | tf_op jit(solution)/shard_map/jat,tc->cja/dot_general | solution.py:127
  12.6 3.5 %fusion.9 = (f32[8,128]{1,0:T(8,128)S(1)}, f32[16,1,64,8,128]{4,2,1,0,3:T(8,128)}) fusion(f32[16,2,64,8,128]{4,2,1,0,3:T(8,128)S(1)} %bitcast.45), kind=kLoop, calls=%fused_computation.24 | loop fusion | flops 4193280 | bytes 12587008 | tf_op jit(solution)/shard_map/reduce_sum | solution.py:59
  16.1 16.6 %multiply_maximum_fusion = f32[1024,8,128]{2,0,1:T(8,128)S(1)} fusion(f32[1024,8,128]{2,0,1:T(8,128)} %bitcast.48, f32[8,128]{1,0:T(8,128)S(1)} %multiply_add_fusion), kind=kLoop, calls=%fused_computation.8 | loop fusion | flops 10485760 | bytes 8392704 | tf_op jit(solution)/shard_map/max | solution.py:60
  36.2 3.3 %copy.12 = bf16[4,2,2,2,32,8,128]{6,5,4,3,2,1,0:T(8,128)(2,1)S(1)} copy(bf16[4,2,2,2,32,8,128]{6,4,3,2,1,0,5:T(8,128)(2,1)S(1)} %bitcast.63) | data formatting | bytes 4194304 | tf_op jit(solution)/shard_map/reshape;squeeze | solution.py:142
  41.4 6.4 %all-to-all-start.2 = ((bf16[1024,8,128]{2,1,0:T(8,128)(2,1)}), bf16[1024,8,128]{2,1,0:T(8,128)(2,1)S(1)}, u32[]{:S(2)}, u32[]{:S(2)}) async-start(bf16[1024,8,128]{2,1,0:T(8,128)(2,1)} %bitcast.53), calls=%async_computation.2 | async-start | bytes 4194304 | tf_op jit(solution)/shard_map/all_to_all | solution.py:148
  47.8 4.9 %copy.7 = bf16[4,2,2,2,32,8,128]{6,5,4,3,2,1,0:T(8,128)(2,1)S(1)} copy(bf16[4,2,2,2,32,8,128]{6,4,3,2,1,0,5:T(8,128)(2,1)} %bitcast.62) | data formatting | bytes 4194304 | tf_op jit(solution)/shard_map/reshape;squeeze | solution.py:142
  54.7 21.0 %all-to-all-done.2 = bf16[1024,8,128]{2,1,0:T(8,128)(2,1)S(1)} async-done(((bf16[1024,8,128]{2,1,0:T(8,128)(2,1)}), bf16[1024,8,128]{2,1,0:T(8,128)(2,1)S(1)}, u32[]{:S(2)}, u32[]{:S(2)}) %all-to-all-start.2) | async-done | bytes 2097184 | tf_op jit(solution)/shard_map/all_to_all | solution.py:148
  77.0 3.7 %all-to-all-start = ((bf16[1024,8,128]{2,1,0:T(8,128)(2,1)}), bf16[1024,8,128]{2,1,0:T(8,128)(2,1)S(1)}, u32[]{:S(2)}, u32[]{:S(2)}) async-start(bf16[1024,8,128]{2,1,0:T(8,128)(2,1)} %bitcast.7), calls=%async_computation | async-start | bytes 4194304 | tf_op jit(solution)/shard_map/all_to_all | solution.py:148
  80.7 3.5 %copy.23 = bf16[64,16,8,128]{3,2,1,0:T(8,128)(2,1)} copy(bf16[64,16,8,128]{3,2,0,1:T(8,128)(2,1)} %bitcast.52) | data formatting | bytes 4194304 | tf_op jit(solution)/shard_map/all_to_all | solution.py:148
  84.2 4.1 %copy.15 = bf16[64,128,128]{2,1,0:T(8,128)(2,1)} copy(bf16[64,128,128]{1,2,0:T(8,128)(2,1)} %bitcast.54) | data formatting | bytes 4194304 | tf_op jit(solution)/shard_map/transpose | solution.py:149
  88.3 4.1 %collective-permute-start.2 = (bf16[2,32,128,128]{3,2,1,0:T(8,128)(2,1)}, bf16[2,32,128,128]{3,2,1,0:T(8,128)(2,1)}, u32[]{:S(2)}, u32[]{:S(2)}) collective-permute-start(bf16[2,32,128,128]{3,2,1,0:T(8,128)(2,1)} %bitcast.56), channel_id=1, source_target_pairs={{16,0},{32,16},{48,32},{80,64},{96,80},{112,96},{17,1},{33,17},{49... | collective-permute-start | bytes 6291464 | tf_op jit(solution)/shard_map/ppermute | solution.py:150
  93.6 14.9 %all-to-all-done = bf16[1024,8,128]{2,1,0:T(8,128)(2,1)S(1)} async-done(((bf16[1024,8,128]{2,1,0:T(8,128)(2,1)}), bf16[1024,8,128]{2,1,0:T(8,128)(2,1)S(1)}, u32[]{:S(2)}, u32[]{:S(2)}) %all-to-all-start) | async-done | bytes 2097184 | tf_op jit(solution)/shard_map/all_to_all | solution.py:148
  113.7 4.1 %collective-permute-start = (bf16[2,32,128,128]{3,2,1,0:T(8,128)(2,1)S(1)}, bf16[2,32,128,128]{3,2,1,0:T(8,128)(2,1)}, u32[]{:S(2)}, u32[]{:S(2)}) collective-permute-start(bf16[2,32,128,128]{3,2,1,0:T(8,128)(2,1)S(1)} %bitcast.59), channel_id=1, source_target_pairs={{16,0},{32,16},{48,32},{80,64},{96,80},{112,96},{17,1},{33,17},{49... | collective-permute-start | bytes 6291464 | tf_op jit(solution)/shard_map/ppermute | solution.py:150
  119.1 18.3 %collective-permute-done.2.next_ref = bf16[2,32,128,128]{3,2,1,0:T(8,128)(2,1)} collective-permute-done((bf16[2,32,128,128]{3,2,1,0:T(8,128)(2,1)}, bf16[2,32,128,128]{3,2,1,0:T(8,128)(2,1)}, u32[]{:S(2)}, u32[]{:S(2)}) %collective-permute-start.2) | collective-permute-done | bytes 2097184 | tf_op jit(solution)/shard_map/ppermute | solution.py:150
  137.3 9.0 %collective-permute-done.3.wrap_ref = bf16[2,32,128,128]{3,2,1,0:T(8,128)(2,1)} collective-permute-done((bf16[2,32,128,128]{3,2,1,0:T(8,128)(2,1)}, bf16[2,32,128,128]{3,2,1,0:T(8,128)(2,1)}, u32[]{:S(2)}, u32[]{:S(2)}) %collective-permute-start.3) | collective-permute-done | bytes 2097184 | tf_op jit(solution)/shard_map/ppermute | solution.py:151
  146.4 16.9 %shard_map.47 = bf16[16,2,32,8,128]{4,3,2,1,0:T(8,128)(2,1)} custom-call(bf16[2,32,128,128]{3,2,1,0:T(8,128)(2,1)} %bitcast.58, bf16[2,32,128,128]{3,2,1,0:T(8,128)(2,1)} %collective-permute-done.2.next_ref, bf16[2,32,128,128]{3,2,1,0:T(8,128)(2,1)} %collective-permute-done.3.wrap_ref), custom_call_target="tpu_custom_call" | custom-call | tf_op jit(solution)/shard_map/pallas_call | solution.py:100
  163.3 4.8 %all-to-all-start.3 = ((bf16[16,2,32,8,128]{4,3,2,1,0:T(8,128)(2,1)}), bf16[16,2,32,8,128]{4,3,2,1,0:T(8,128)(2,1)}, u32[]{:S(2)}, u32[]{:S(2)}) async-start(bf16[16,2,32,8,128]{4,3,2,1,0:T(8,128)(2,1)} %shard_map.47), calls=%async_computation.3 | async-start | bytes 4194304 | tf_op jit(solution)/shard_map/all_to_all | solution.py:153
  168.1 13.4 %collective-permute-done.next_ref = bf16[2,32,128,128]{3,2,1,0:T(8,128)(2,1)} collective-permute-done((bf16[2,32,128,128]{3,2,1,0:T(8,128)(2,1)S(1)}, bf16[2,32,128,128]{3,2,1,0:T(8,128)(2,1)}, u32[]{:S(2)}, u32[]{:S(2)}) %collective-permute-start) | collective-permute-done | bytes 2097184 | tf_op jit(solution)/shard_map/ppermute | solution.py:150
  181.5 8.9 %collective-permute-done.1.wrap_ref = bf16[2,32,128,128]{3,2,1,0:T(8,128)(2,1)} collective-permute-done((bf16[2,32,128,128]{3,2,1,0:T(8,128)(2,1)S(1)}, bf16[2,32,128,128]{3,2,1,0:T(8,128)(2,1)}, u32[]{:S(2)}, u32[]{:S(2)}) %collective-permute-start.1) | collective-permute-done | bytes 2097184 | tf_op jit(solution)/shard_map/ppermute | solution.py:151
  190.3 16.9 %shard_map.46 = bf16[16,2,32,8,128]{4,3,2,1,0:T(8,128)(2,1)} custom-call(bf16[2,32,128,128]{3,2,1,0:T(8,128)(2,1)} %bitcast.61, bf16[2,32,128,128]{3,2,1,0:T(8,128)(2,1)} %collective-permute-done.next_ref, bf16[2,32,128,128]{3,2,1,0:T(8,128)(2,1)} %collective-permute-done.1.wrap_ref), custom_call_target="tpu_custom_call" | custom-call | tf_op jit(solution)/shard_map/pallas_call | solution.py:100
  207.3 4.6 %all-to-all-start.1 = ((bf16[16,2,32,8,128]{4,3,2,1,0:T(8,128)(2,1)}), bf16[16,2,32,8,128]{4,3,2,1,0:T(8,128)(2,1)S(1)}, u32[]{:S(2)}, u32[]{:S(2)}) async-start(bf16[16,2,32,8,128]{4,3,2,1,0:T(8,128)(2,1)} %shard_map.46), calls=%async_computation.1 | async-start | bytes 4194304 | tf_op jit(solution)/shard_map/all_to_all | solution.py:153
  219.0 8.5 %fusion.6 = f32[8,128,2048]{2,1,0:T(8,128)} fusion(bf16[1024,2048,1]{1,0,2:T(8,128)(2,1)S(1)} %bitcast.64, bf16[1024,8,128]{2,1,0:T(8,128)(2,1)} %bitcast.23), kind=kOutput, calls=%fused_computation.18 | convolution fusion | flops 4294967296 | bytes 14680064 | tf_op jit(solution)/shard_map/hak,hl->akl/dot_general | solution.py:156
  227.5 12.2 %all-to-all-done.1 = bf16[16,2,32,8,128]{4,3,2,1,0:T(8,128)(2,1)S(1)} async-done(((bf16[16,2,32,8,128]{4,3,2,1,0:T(8,128)(2,1)}), bf16[16,2,32,8,128]{4,3,2,1,0:T(8,128)(2,1)S(1)}, u32[]{:S(2)}, u32[]{:S(2)}) %all-to-all-start.1) | async-done | bytes 2097184 | tf_op jit(solution)/shard_map/all_to_all | solution.py:153
  239.7 9.6 %add_convert_fusion = bf16[8,128,2048]{2,1,0:T(8,128)(2,1)} fusion(f32[8,128,2048]{2,1,0:T(8,128)} %fusion.6, bf16[1024,2048,1]{1,0,2:T(8,128)(2,1)} %bitcast.49, bf16[1024,8,128]{2,1,0:T(8,128)(2,1)S(1)} %bitcast.50), kind=kOutput, calls=%fused_computation.3 | convolution fusion | flops 4299161600 | bytes 18874368 | tf_op jit(solution)/shard_map/hak,hl->akl/dot_general | solution.py:156
  (23 shorter events, 23.5 us)
Async XLA Ops:
  12.6 3.5 %copy-start.4 = (s32[128]{0:T(128)S(1)}, s32[128]{0:T(128)}, u32[]{:S(2)}) copy-start(s32[128]{0:T(128)} %param.5) | copy-start | bytes 1540
  41.4 34.3 %all-to-all-start.2 = ((bf16[1024,8,128]{2,1,0:T(8,128)(2,1)}), bf16[1024,8,128]{2,1,0:T(8,128)(2,1)S(1)}, u32[]{:S(2)}, u32[]{:S(2)}) async-start(bf16[1024,8,128]{2,1,0:T(8,128)(2,1)} %bitcast.53), calls=%async_computation.2 | async-start | bytes 4194304 | tf_op jit(solution)/shard_map/all_to_all | solution.py:148
  75.7 1.3 copy-start
  77.0 31.5 %all-to-all-start = ((bf16[1024,8,128]{2,1,0:T(8,128)(2,1)}), bf16[1024,8,128]{2,1,0:T(8,128)(2,1)S(1)}, u32[]{:S(2)}, u32[]{:S(2)}) async-start(bf16[1024,8,128]{2,1,0:T(8,128)(2,1)} %bitcast.7), calls=%async_computation | async-start | bytes 4194304 | tf_op jit(solution)/shard_map/all_to_all | solution.py:148
  88.3 49.0 %collective-permute-start.2 = (bf16[2,32,128,128]{3,2,1,0:T(8,128)(2,1)}, bf16[2,32,128,128]{3,2,1,0:T(8,128)(2,1)}, u32[]{:S(2)}, u32[]{:S(2)}) collective-permute-start(bf16[2,32,128,128]{3,2,1,0:T(8,128)(2,1)} %bitcast.56), channel_id=1, source_target_pairs={{16,0},{32,16},{48,32},{80,64},{96,80},{112,96},{17,1},{33,17},{49... | collective-permute-start | bytes 6291464 | tf_op jit(solution)/shard_map/ppermute | solution.py:150
  92.3 54.0 %collective-permute-start.3 = (bf16[2,32,128,128]{3,2,1,0:T(8,128)(2,1)}, bf16[2,32,128,128]{3,2,1,0:T(8,128)(2,1)}, u32[]{:S(2)}, u32[]{:S(2)}) collective-permute-start(bf16[2,32,128,128]{3,2,1,0:T(8,128)(2,1)} %bitcast.57), channel_id=1, source_target_pairs={{64,50},{65,51},{66,48},{67,49},{68,54},{69,55},{70,52},{71,53},{7... | collective-permute-start | bytes 6291464 | tf_op jit(solution)/shard_map/ppermute | solution.py:151
  113.7 49.7 %copy-start.1 = (bf16[64,128,128]{2,1,0:T(8,128)(2,1)}, bf16[64,128,128]{2,1,0:T(8,128)(2,1)S(1)}, u32[]{:S(2)}) copy-start(bf16[64,128,128]{2,1,0:T(8,128)(2,1)S(1)} %copy.10) | copy-start | bytes 6291460
  113.7 67.8 %collective-permute-start = (bf16[2,32,128,128]{3,2,1,0:T(8,128)(2,1)S(1)}, bf16[2,32,128,128]{3,2,1,0:T(8,128)(2,1)}, u32[]{:S(2)}, u32[]{:S(2)}) collective-permute-start(bf16[2,32,128,128]{3,2,1,0:T(8,128)(2,1)S(1)} %bitcast.59), channel_id=1, source_target_pairs={{16,0},{32,16},{48,32},{80,64},{96,80},{112,96},{17,1},{33,17},{49... | collective-permute-start | bytes 6291464 | tf_op jit(solution)/shard_map/ppermute | solution.py:150
  117.8 72.6 %collective-permute-start.1 = (bf16[2,32,128,128]{3,2,1,0:T(8,128)(2,1)S(1)}, bf16[2,32,128,128]{3,2,1,0:T(8,128)(2,1)}, u32[]{:S(2)}, u32[]{:S(2)}) collective-permute-start(bf16[2,32,128,128]{3,2,1,0:T(8,128)(2,1)S(1)} %bitcast.60), channel_id=1, source_target_pairs={{64,50},{65,51},{66,48},{67,49},{68,54},{69,55},{70,52},{71,53},{7... | collective-permute-start | bytes 6291464 | tf_op jit(solution)/shard_map/ppermute | solution.py:151
  163.3 44.0 %all-to-all-start.3 = ((bf16[16,2,32,8,128]{4,3,2,1,0:T(8,128)(2,1)}), bf16[16,2,32,8,128]{4,3,2,1,0:T(8,128)(2,1)}, u32[]{:S(2)}, u32[]{:S(2)}) async-start(bf16[16,2,32,8,128]{4,3,2,1,0:T(8,128)(2,1)} %shard_map.47), calls=%async_computation.3 | async-start | bytes 4194304 | tf_op jit(solution)/shard_map/all_to_all | solution.py:153
  207.3 32.4 %all-to-all-start.1 = ((bf16[16,2,32,8,128]{4,3,2,1,0:T(8,128)(2,1)}), bf16[16,2,32,8,128]{4,3,2,1,0:T(8,128)(2,1)S(1)}, u32[]{:S(2)}, u32[]{:S(2)}) async-start(bf16[16,2,32,8,128]{4,3,2,1,0:T(8,128)(2,1)} %shard_map.46), calls=%async_computation.1 | async-start | bytes 4194304 | tf_op jit(solution)/shard_map/all_to_all | solution.py:153
  211.9 3.5 %copy-start.2 = (bf16[4,2,2,2,32,2048]{5,4,3,2,1,0:T(8,128)(2,1)S(1)}, bf16[4,2,2,2,32,2048]{5,4,3,2,1,0:T(8,128)(2,1)}, u32[]{:S(2)}) copy-start(bf16[4,2,2,2,32,2048]{5,4,3,2,1,0:T(8,128)(2,1)} %constant.33) | copy-start | bytes 12582916
  211.9 4.7 %copy-start.3 = (bf16[4,2,2,2,32,2048]{5,4,3,2,1,0:T(8,128)(2,1)S(1)}, bf16[4,2,2,2,32,2048]{5,4,3,2,1,0:T(8,128)(2,1)}, u32[]{:S(2)}) copy-start(bf16[4,2,2,2,32,2048]{5,4,3,2,1,0:T(8,128)(2,1)} %constant.34) | copy-start | bytes 12582916

commit v2 on v1

--- a/solution.py
+++ b/solution.py
@@ -55,7 +55,8 @@
     imag_part = split[:, 1].reshape((bins,) + rest)
     amplitude = jnp.sqrt(real_part * real_part + imag_part * imag_part)
     padded = jnp.pad(amplitude, [(SMOOTH, SMOOTH)] + [(0, 0)] * len(rest))
-    smooth = sum((padded[i : i + bins] for i in range(2 * SMOOTH + 1))) / (2 * SMOOTH + 1)
+    triple = padded[: bins + 6] + padded[1 : bins + 7] + padded[2 : bins + 8]
+    smooth = (triple[:bins] + triple[3 : bins + 3] + triple[6 : bins + 6]) / (2 * SMOOTH + 1)
     water = 0.8 * jnp.mean(amplitude, axis=0, keepdims=True) + 1e-06
     level = jnp.maximum(smooth, water).reshape((groups, 1, width) + rest)
     return (split / level).reshape(spectra.shape)

time: 250 us -> 234 us (0.936)
  other arithmetic: 30.4 us -> 14.1 us
    max x1, other arithmetic: 16.6 us -> 1.09 us  [whiten_cols(): level = jnp.maximum(smooth, water).reshape((groups, 1, width) + rest)]
  transfers between devices with their start and end apart: 8 -> 8, of which waited for: 7 -> 7; matrix products, arithmetic and copies ran while one was open for 13% -> 14% of each run, Pallas kernels for 14% -> 15%
where the time goes in v2:
time: 234 us; the launch traced here: 233 us
  waiting for transfers between devices  97.5 us (42%)
  Pallas kernels  33.9 us (14%)
  matrix products  30.7 us (13%)
  starting transfers between devices  30.2 us (13%)
  local copies, waits for them, and re-layouts  26.4 us (11%)
  other arithmetic  14.1 us (6%)
    all_to_all x2, waiting for transfers between devices, body(): own = lax.all_to_all(piece, 'tm', split_axis=0, concat_axis=1, tiled=True)  35.8 us
    pallas_call x2, Pallas kernels, cross(): pl.pallas_call(cross_kernel, grid=(width // step,), in_specs=[spec, spec,...  33.9 us
    ppermute x2, waiting for transfers between devices, body(): next_t = lax.ppermute(own_t, 'chan', inner_route)  31.6 us
    dot_general x2, matrix products, body(): jnp.einsum('hak,hl->akl', gathered, rows, preferred_element_type=jnp.floa...  18.1 us
    ppermute x2, waiting for transfers between devices, body(): wrap_t = lax.ppermute(own_t, ('chan', 'tm'), wrap_route)  17.9 us
    dot_general x1, matrix products, body(): jnp.einsum('jat,tc->cja', traces, table, preferred_element_type=jnp.float32)  12.5 us
    all_to_all x2, waiting for transfers between devices, body(): lax.all_to_all(stack, 'tm', split_axis=0, concat_axis=0, tiled=True)  12.2 us
    all_to_all x2, starting transfers between devices, body(): own = lax.all_to_all(piece, 'tm', split_axis=0, concat_axis=1, tiled=True)  10.2 us
  transfers between devices with their start and end apart: 8, of which 7 were waited for; matrix products, arithmetic and copies ran while one was open for 14% of the time, Pallas kernels for 15%

profile of v2, /device:TPU:6, one launch (start us, length us, event | category | flops | bytes accessed | tf_op | source)
XLA Modules:
  0.0 233.0 jit_solution(9799105874160818616)
XLA Ops:
  0.0 12.5 %fusion.12 = f32[2048,8,128]{2,0,1:T(8,128)S(1)} fusion(bf16[2048,2048,1]{0,1,2:T(8,128)(2,1)} %constant.38, bf16[8,128,2048]{2,1,0:T(8,128)(2,1)} %param.4), kind=kOutput, calls=%fused_computation.25 | convolution fusion | flops 8589934592 | bytes 20971520 | tf_op jit(solution)/shard_map/jat,tc->cja/dot_general | solution.py:128
  19.8 3.3 %copy.12 = bf16[4,2,2,2,32,8,128]{6,5,4,3,2,1,0:T(8,128)(2,1)S(1)} copy(bf16[4,2,2,2,32,8,128]{6,4,3,2,1,0,5:T(8,128)(2,1)S(1)} %bitcast.63) | data formatting | bytes 4194304 | tf_op jit(solution)/shard_map/reshape;squeeze | solution.py:143
  25.1 6.4 %all-to-all-start.2 = ((bf16[1024,8,128]{2,1,0:T(8,128)(2,1)}), bf16[1024,8,128]{2,1,0:T(8,128)(2,1)S(1)}, u32[]{:S(2)}, u32[]{:S(2)}) async-start(bf16[1024,8,128]{2,1,0:T(8,128)(2,1)} %bitcast.53), calls=%async_computation.2 | async-start | bytes 4194304 | tf_op jit(solution)/shard_map/all_to_all | solution.py:149
  31.5 4.9 %copy.7 = bf16[4,2,2,2,32,8,128]{6,5,4,3,2,1,0:T(8,128)(2,1)S(1)} copy(bf16[4,2,2,2,32,8,128]{6,4,3,2,1,0,5:T(8,128)(2,1)} %bitcast.62) | data formatting | bytes 4194304 | tf_op jit(solution)/shard_map/reshape;squeeze | solution.py:143
  38.3 21.0 %all-to-all-done.2 = bf16[1024,8,128]{2,1,0:T(8,128)(2,1)S(1)} async-done(((bf16[1024,8,128]{2,1,0:T(8,128)(2,1)}), bf16[1024,8,128]{2,1,0:T(8,128)(2,1)S(1)}, u32[]{:S(2)}, u32[]{:S(2)}) %all-to-all-start.2) | async-done | bytes 2097184 | tf_op jit(solution)/shard_map/all_to_all | solution.py:149
  60.6 3.7 %all-to-all-start = ((bf16[1024,8,128]{2,1,0:T(8,128)(2,1)}), bf16[1024,8,128]{2,1,0:T(8,128)(2,1)S(1)}, u32[]{:S(2)}, u32[]{:S(2)}) async-start(bf16[1024,8,128]{2,1,0:T(8,128)(2,1)} %bitcast.7), calls=%async_computation | async-start | bytes 4194304 | tf_op jit(solution)/shard_map/all_to_all | solution.py:149
  64.4 3.5 %copy.23 = bf16[64,16,8,128]{3,2,1,0:T(8,128)(2,1)} copy(bf16[64,16,8,128]{3,2,0,1:T(8,128)(2,1)} %bitcast.52) | data formatting | bytes 4194304 | tf_op jit(solution)/shard_map/all_to_all | solution.py:149
  67.9 4.1 %copy.15 = bf16[64,128,128]{2,1,0:T(8,128)(2,1)} copy(bf16[64,128,128]{1,2,0:T(8,128)(2,1)} %bitcast.54) | data formatting | bytes 4194304 | tf_op jit(solution)/shard_map/transpose | solution.py:150
  71.9 4.1 %collective-permute-start.2 = (bf16[2,32,128,128]{3,2,1,0:T(8,128)(2,1)}, bf16[2,32,128,128]{3,2,1,0:T(8,128)(2,1)}, u32[]{:S(2)}, u32[]{:S(2)}) collective-permute-start(bf16[2,32,128,128]{3,2,1,0:T(8,128)(2,1)} %bitcast.56), channel_id=1, source_target_pairs={{16,0},{32,16},{48,32},{80,64},{96,80},{112,96},{17,1},{33,17},{49... | collective-permute-start | bytes 6291464 | tf_op jit(solution)/shard_map/ppermute | solution.py:151
  77.3 14.9 %all-to-all-done = bf16[1024,8,128]{2,1,0:T(8,128)(2,1)S(1)} async-done(((bf16[1024,8,128]{2,1,0:T(8,128)(2,1)}), bf16[1024,8,128]{2,1,0:T(8,128)(2,1)S(1)}, u32[]{:S(2)}, u32[]{:S(2)}) %all-to-all-start) | async-done | bytes 2097184 | tf_op jit(solution)/shard_map/all_to_all | solution.py:149
  94.1 3.2 %copy.10 = bf16[64,128,128]{2,1,0:T(8,128)(2,1)S(1)} copy(bf16[64,128,128]{1,2,0:T(8,128)(2,1)} %bitcast.55) | data formatting | bytes 4194304 | tf_op jit(solution)/shard_map/transpose | solution.py:150
  97.3 4.1 %collective-permute-start = (bf16[2,32,128,128]{3,2,1,0:T(8,128)(2,1)S(1)}, bf16[2,32,128,128]{3,2,1,0:T(8,128)(2,1)}, u32[]{:S(2)}, u32[]{:S(2)}) collective-permute-start(bf16[2,32,128,128]{3,2,1,0:T(8,128)(2,1)S(1)} %bitcast.59), channel_id=1, source_target_pairs={{16,0},{32,16},{48,32},{80,64},{96,80},{112,96},{17,1},{33,17},{49... | collective-permute-start | bytes 6291464 | tf_op jit(solution)/shard_map/ppermute | solution.py:151
  102.7 18.3 %collective-permute-done.2.next_ref = bf16[2,32,128,128]{3,2,1,0:T(8,128)(2,1)} collective-permute-done((bf16[2,32,128,128]{3,2,1,0:T(8,128)(2,1)}, bf16[2,32,128,128]{3,2,1,0:T(8,128)(2,1)}, u32[]{:S(2)}, u32[]{:S(2)}) %collective-permute-start.2) | collective-permute-done | bytes 2097184 | tf_op jit(solution)/shard_map/ppermute | solution.py:151
  121.0 9.0 %collective-permute-done.3.wrap_ref = bf16[2,32,128,128]{3,2,1,0:T(8,128)(2,1)} collective-permute-done((bf16[2,32,128,128]{3,2,1,0:T(8,128)(2,1)}, bf16[2,32,128,128]{3,2,1,0:T(8,128)(2,1)}, u32[]{:S(2)}, u32[]{:S(2)}) %collective-permute-start.3) | collective-permute-done | bytes 2097184 | tf_op jit(solution)/shard_map/ppermute | solution.py:152
  130.0 16.9 %shard_map.47 = bf16[16,2,32,8,128]{4,3,2,1,0:T(8,128)(2,1)} custom-call(bf16[2,32,128,128]{3,2,1,0:T(8,128)(2,1)} %bitcast.58, bf16[2,32,128,128]{3,2,1,0:T(8,128)(2,1)} %collective-permute-done.2.next_ref, bf16[2,32,128,128]{3,2,1,0:T(8,128)(2,1)} %collective-permute-done.3.wrap_ref), custom_call_target="tpu_custom_call" | custom-call | tf_op jit(solution)/shard_map/pallas_call | solution.py:101
  147.0 4.8 %all-to-all-start.3 = ((bf16[16,2,32,8,128]{4,3,2,1,0:T(8,128)(2,1)}), bf16[16,2,32,8,128]{4,3,2,1,0:T(8,128)(2,1)}, u32[]{:S(2)}, u32[]{:S(2)}) async-start(bf16[16,2,32,8,128]{4,3,2,1,0:T(8,128)(2,1)} %shard_map.47), calls=%async_computation.3 | async-start | bytes 4194304 | tf_op jit(solution)/shard_map/all_to_all | solution.py:154
  151.8 13.4 %collective-permute-done.next_ref = bf16[2,32,128,128]{3,2,1,0:T(8,128)(2,1)} collective-permute-done((bf16[2,32,128,128]{3,2,1,0:T(8,128)(2,1)S(1)}, bf16[2,32,128,128]{3,2,1,0:T(8,128)(2,1)}, u32[]{:S(2)}, u32[]{:S(2)}) %collective-permute-start) | collective-permute-done | bytes 2097184 | tf_op jit(solution)/shard_map/ppermute | solution.py:151
  165.1 8.9 %collective-permute-done.1.wrap_ref = bf16[2,32,128,128]{3,2,1,0:T(8,128)(2,1)} collective-permute-done((bf16[2,32,128,128]{3,2,1,0:T(8,128)(2,1)S(1)}, bf16[2,32,128,128]{3,2,1,0:T(8,128)(2,1)}, u32[]{:S(2)}, u32[]{:S(2)}) %collective-permute-start.1) | collective-permute-done | bytes 2097184 | tf_op jit(solution)/shard_map/ppermute | solution.py:152
  174.0 16.9 %shard_map.46 = bf16[16,2,32,8,128]{4,3,2,1,0:T(8,128)(2,1)} custom-call(bf16[2,32,128,128]{3,2,1,0:T(8,128)(2,1)} %bitcast.61, bf16[2,32,128,128]{3,2,1,0:T(8,128)(2,1)} %collective-permute-done.next_ref, bf16[2,32,128,128]{3,2,1,0:T(8,128)(2,1)} %collective-permute-done.1.wrap_ref), custom_call_target="tpu_custom_call" | custom-call | tf_op jit(solution)/shard_map/pallas_call | solution.py:101
  190.9 4.6 %all-to-all-start.1 = ((bf16[16,2,32,8,128]{4,3,2,1,0:T(8,128)(2,1)}), bf16[16,2,32,8,128]{4,3,2,1,0:T(8,128)(2,1)S(1)}, u32[]{:S(2)}, u32[]{:S(2)}) async-start(bf16[16,2,32,8,128]{4,3,2,1,0:T(8,128)(2,1)} %shard_map.46), calls=%async_computation.1 | async-start | bytes 4194304 | tf_op jit(solution)/shard_map/all_to_all | solution.py:154
  195.5 2.8 %broadcast_select_fusion = bf16[4,2,2,2,32,2048]{5,4,3,2,1,0:T(8,128)(2,1)S(1)} fusion(bf16[4,2,2,2,32,2048]{5,4,3,2,1,0:T(8,128)(2,1)} %constant.37, bf16[4,2,2,2,32,2048]{5,4,3,2,1,0:T(8,128)(2,1)} %constant.36, pred[]{:T(512)S(6)} %lt.3), kind=kLoop, calls=%fused_computation.13 | loop fusion | flops 2097152 | bytes 12582913 | tf_op jit(solution)/shard_map/jit(_where)/select_n | solution.py:144
  202.7 8.5 %fusion.6 = f32[8,128,2048]{2,1,0:T(8,128)} fusion(bf16[1024,2048,1]{1,0,2:T(8,128)(2,1)S(1)} %bitcast.64, bf16[1024,8,128]{2,1,0:T(8,128)(2,1)} %bitcast.23), kind=kOutput, calls=%fused_computation.17 | convolution fusion | flops 4294967296 | bytes 14680064 | tf_op jit(solution)/shard_map/hak,hl->akl/dot_general | solution.py:157
  211.2 12.2 %all-to-all-done.1 = bf16[16,2,32,8,128]{4,3,2,1,0:T(8,128)(2,1)S(1)} async-done(((bf16[16,2,32,8,128]{4,3,2,1,0:T(8,128)(2,1)}), bf16[16,2,32,8,128]{4,3,2,1,0:T(8,128)(2,1)S(1)}, u32[]{:S(2)}, u32[]{:S(2)}) %all-to-all-start.1) | async-done | bytes 2097184 | tf_op jit(solution)/shard_map/all_to_all | solution.py:154
  223.3 9.6 %add_convert_fusion = bf16[8,128,2048]{2,1,0:T(8,128)(2,1)} fusion(f32[8,128,2048]{2,1,0:T(8,128)} %fusion.6, bf16[1024,2048,1]{1,0,2:T(8,128)(2,1)} %bitcast.49, bf16[1024,8,128]{2,1,0:T(8,128)(2,1)S(1)} %bitcast.50), kind=kOutput, calls=%fused_computation.3 | convolution fusion | flops 4299161600 | bytes 18874368 | tf_op jit(solution)/shard_map/hak,hl->akl/dot_general | solution.py:157
  (24 shorter events, 21.2 us)
Async XLA Ops:
  14.2 1.1 copy-start.4
  25.1 34.3 %all-to-all-start.2 = ((bf16[1024,8,128]{2,1,0:T(8,128)(2,1)}), bf16[1024,8,128]{2,1,0:T(8,128)(2,1)S(1)}, u32[]{:S(2)}, u32[]{:S(2)}) async-start(bf16[1024,8,128]{2,1,0:T(8,128)(2,1)} %bitcast.53), calls=%async_computation.2 | async-start | bytes 4194304 | tf_op jit(solution)/shard_map/all_to_all | solution.py:149
  59.3 1.3 copy-start
  60.6 31.5 %all-to-all-start = ((bf16[1024,8,128]{2,1,0:T(8,128)(2,1)}), bf16[1024,8,128]{2,1,0:T(8,128)(2,1)S(1)}, u32[]{:S(2)}, u32[]{:S(2)}) async-start(bf16[1024,8,128]{2,1,0:T(8,128)(2,1)} %bitcast.7), calls=%async_computation | async-start | bytes 4194304 | tf_op jit(solution)/shard_map/all_to_all | solution.py:149
  71.9 49.0 %collective-permute-start.2 = (bf16[2,32,128,128]{3,2,1,0:T(8,128)(2,1)}, bf16[2,32,128,128]{3,2,1,0:T(8,128)(2,1)}, u32[]{:S(2)}, u32[]{:S(2)}) collective-permute-start(bf16[2,32,128,128]{3,2,1,0:T(8,128)(2,1)} %bitcast.56), channel_id=1, source_target_pairs={{16,0},{32,16},{48,32},{80,64},{96,80},{112,96},{17,1},{33,17},{49... | collective-permute-start | bytes 6291464 | tf_op jit(solution)/shard_map/ppermute | solution.py:151
  76.0 54.0 %collective-permute-start.3 = (bf16[2,32,128,128]{3,2,1,0:T(8,128)(2,1)}, bf16[2,32,128,128]{3,2,1,0:T(8,128)(2,1)}, u32[]{:S(2)}, u32[]{:S(2)}) collective-permute-start(bf16[2,32,128,128]{3,2,1,0:T(8,128)(2,1)} %bitcast.57), channel_id=1, source_target_pairs={{64,50},{65,51},{66,48},{67,49},{68,54},{69,55},{70,52},{71,53},{7... | collective-permute-start | bytes 6291464 | tf_op jit(solution)/shard_map/ppermute | solution.py:152
  97.3 49.6 %copy-start.1 = (bf16[64,128,128]{2,1,0:T(8,128)(2,1)}, bf16[64,128,128]{2,1,0:T(8,128)(2,1)S(1)}, u32[]{:S(2)}) copy-start(bf16[64,128,128]{2,1,0:T(8,128)(2,1)S(1)} %copy.10) | copy-start | bytes 6291460
  97.3 67.8 %collective-permute-start = (bf16[2,32,128,128]{3,2,1,0:T(8,128)(2,1)S(1)}, bf16[2,32,128,128]{3,2,1,0:T(8,128)(2,1)}, u32[]{:S(2)}, u32[]{:S(2)}) collective-permute-start(bf16[2,32,128,128]{3,2,1,0:T(8,128)(2,1)S(1)} %bitcast.59), channel_id=1, source_target_pairs={{16,0},{32,16},{48,32},{80,64},{96,80},{112,96},{17,1},{33,17},{49... | collective-permute-start | bytes 6291464 | tf_op jit(solution)/shard_map/ppermute | solution.py:151
  101.4 72.6 %collective-permute-start.1 = (bf16[2,32,128,128]{3,2,1,0:T(8,128)(2,1)S(1)}, bf16[2,32,128,128]{3,2,1,0:T(8,128)(2,1)}, u32[]{:S(2)}, u32[]{:S(2)}) collective-permute-start(bf16[2,32,128,128]{3,2,1,0:T(8,128)(2,1)S(1)} %bitcast.60), channel_id=1, source_target_pairs={{64,50},{65,51},{66,48},{67,49},{68,54},{69,55},{70,52},{71,53},{7... | collective-permute-start | bytes 6291464 | tf_op jit(solution)/shard_map/ppermute | solution.py:152
  147.0 44.0 %all-to-all-start.3 = ((bf16[16,2,32,8,128]{4,3,2,1,0:T(8,128)(2,1)}), bf16[16,2,32,8,128]{4,3,2,1,0:T(8,128)(2,1)}, u32[]{:S(2)}, u32[]{:S(2)}) async-start(bf16[16,2,32,8,128]{4,3,2,1,0:T(8,128)(2,1)} %shard_map.47), calls=%async_computation.3 | async-start | bytes 4194304 | tf_op jit(solution)/shard_map/all_to_all | solution.py:154
  190.9 32.4 %all-to-all-start.1 = ((bf16[16,2,32,8,128]{4,3,2,1,0:T(8,128)(2,1)}), bf16[16,2,32,8,128]{4,3,2,1,0:T(8,128)(2,1)S(1)}, u32[]{:S(2)}, u32[]{:S(2)}) async-start(bf16[16,2,32,8,128]{4,3,2,1,0:T(8,128)(2,1)} %shard_map.46), calls=%async_computation.1 | async-start | bytes 4194304 | tf_op jit(solution)/shard_map/all_to_all | solution.py:154
  195.5 3.5 %copy-start.2 = (bf16[4,2,2,2,32,2048]{5,4,3,2,1,0:T(8,128)(2,1)S(1)}, bf16[4,2,2,2,32,2048]{5,4,3,2,1,0:T(8,128)(2,1)}, u32[]{:S(2)}) copy-start(bf16[4,2,2,2,32,2048]{5,4,3,2,1,0:T(8,128)(2,1)} %constant.33) | copy-start | bytes 12582916
  195.5 4.7 %copy-start.3 = (bf16[4,2,2,2,32,2048]{5,4,3,2,1,0:T(8,128)(2,1)S(1)}, bf16[4,2,2,2,32,2048]{5,4,3,2,1,0:T(8,128)(2,1)}, u32[]{:S(2)}) copy-start(bf16[4,2,2,2,32,2048]{5,4,3,2,1,0:T(8,128)(2,1)} %constant.34) | copy-start | bytes 12582916

commit v3 on v2

--- a/solution.py
+++ b/solution.py
@@ -119,16 +119,16 @@
     bins = samples // 2
     groups = lax.axis_size("tm")
     group_width = bins // groups
-    width = group_width // CHUNKS
+    widths = (group_width * 5 // 8, group_width * 3 // 8)
     segments = seg_dev * groups
     table = forward_table(samples, bins, group_width)
     inverse = inverse_table(samples, bins, group_width, segments).reshape(
-        groups, 2, CHUNKS, width, samples
+        groups, 2, group_width, samples
     )
     spectra = jnp.einsum("jat,tc->cja", traces, table, preferred_element_type=jnp.float32)
     flags = live.astype(jnp.float32)
     white = (whiten_cols(spectra, groups) * flags).astype(jnp.bfloat16)
-    white = white.reshape(groups, 2, CHUNKS, width, seg_dev, block)
+    white = white.reshape(groups, 2, group_width, seg_dev, block)
     blocks = lax.axis_size("chan")
     inner_route = [(i + 1, i) for i in range(blocks - 1) if (i + 1) % ROW != 0]
     wrap_route = [
@@ -144,8 +144,10 @@
         return jnp.where(swapped, split[:, ::-1], split).reshape(x.shape)
 
     lagged = None
-    for chunk in range(CHUNKS):
-        piece = swap_pairs(white[:, :, chunk]).reshape(groups * 2 * width, seg_dev, block)
+    for chunk, width in enumerate(widths):
+        first = sum(widths[:chunk])
+        piece = swap_pairs(white[:, :, first : first + width])
+        piece = piece.reshape(groups * 2 * width, seg_dev, block)
         own = lax.all_to_all(piece, "tm", split_axis=0, concat_axis=1, tiled=True)
         own_t = jnp.swapaxes(own, 1, 2).reshape(2, width, block, segments)
         next_t = lax.ppermute(own_t, "chan", inner_route)
@@ -153,7 +155,7 @@
         stack = cross(own_t, next_t, wrap_t, groups)
         gathered = lax.all_to_all(stack, "tm", split_axis=0, concat_axis=0, tiled=True)
         gathered = gathered.reshape(groups * 2 * width, block // groups, block)
-        rows = swap_pairs(inverse[:, :, chunk]).reshape(groups * 2 * width, samples)
+        rows = swap_pairs(inverse[:, :, first : first + width]).reshape(groups * 2 * width, samples)
         part = jnp.einsum("hak,hl->akl", gathered, rows, preferred_element_type=jnp.float32)
         lagged = part if lagged is None else lagged + part
     return lagged.astype(jnp.bfloat16)

time: 234 us -> 235 us (level)
  local copies, waits for them, and re-layouts: 26.4 us -> 21.8 us
  waiting for transfers between devices: 97.5 us -> 101 us
    another operation x2 -> x0, local copies, waits for them, and re-layouts: 8.22 us -> none  [swap_pairs(): split = x.reshape((groups // 4, 2, 2) + x.shape[1:])]
    all_to_all x2, waiting for transfers between devices: 12.2 us -> 18.5 us  [body(): lax.all_to_all(stack, 'tm', split_axis=0, concat_axis=0, tiled=True)]
    reshape x0 -> x2, local copies, waits for them, and re-layouts: none -> 4.87 us  [swap_pairs(): split = x.reshape((groups // 4, 2, 2) + x.shape[1:])]
    ppermute x2, waiting for transfers between devices: 31.6 us -> 28.4 us  [body(): next_t = lax.ppermute(own_t, 'chan', inner_route)]
    select_n x4, other arithmetic: 9.02 us -> 11.5 us  [swap_pairs(): return jnp.where(swapped, split[:, ::-1], split).reshape(x.shape)]
  transfers between devices with their start and end apart: 8 -> 8, of which waited for: 7 -> 6; matrix products, arithmetic and copies ran while one was open for 14% -> 14% of each run, Pallas kernels for 15% -> 14%
where the time goes in v3:
time: 235 us; the launch traced here: 234 us
  waiting for transfers between devices  101 us (43%)
  Pallas kernels  34 us (14%)
  matrix products  30.8 us (13%)
  starting transfers between devices  30.3 us (13%)
  local copies, waits for them, and re-layouts  21.8 us (9%)
  other arithmetic  16.4 us (7%)
    all_to_all x2, waiting for transfers between devices, body(): own = lax.all_to_all(piece, 'tm', split_axis=0, concat_axis=1, tiled=True)  37.2 us
    pallas_call x2, Pallas kernels, cross(): pl.pallas_call(cross_kernel, grid=(width // step,), in_specs=[spec, spec,...  34 us
    ppermute x2, waiting for transfers between devices, body(): next_t = lax.ppermute(own_t, 'chan', inner_route)  28.4 us
    all_to_all x2, waiting for transfers between devices, body(): lax.all_to_all(stack, 'tm', split_axis=0, concat_axis=0, tiled=True)  18.5 us
    dot_general x2, matrix products, body(): jnp.einsum('hak,hl->akl', gathered, rows, preferred_element_type=jnp.floa...  18.3 us
    ppermute x2, waiting for transfers between devices, body(): wrap_t = lax.ppermute(own_t, ('chan', 'tm'), wrap_route)  16.7 us
    dot_general x1, matrix products, body(): jnp.einsum('jat,tc->cja', traces, table, preferred_element_type=jnp.float32)  12.5 us
    select_n x4, other arithmetic, swap_pairs(): return jnp.where(swapped, split[:, ::-1], split).reshape(x.shape)  11.5 us
  transfers between devices with their start and end apart: 8, of which 6 were waited for; matrix products, arithmetic and copies ran while one was open for 14% of the time, Pallas kernels for 14%

profile of v3, /device:TPU:6, one launch (start us, length us, event | category | flops | bytes accessed | tf_op | source)
XLA Modules:
  0.0 234.2 jit_solution(7879620037107071695)
XLA Ops:
  0.0 12.5 %fusion.11 = f32[2048,8,128]{2,0,1:T(8,128)S(1)} fusion(bf16[2048,2048,1]{0,1,2:T(8,128)(2,1)} %constant.38, bf16[8,128,2048]{2,1,0:T(8,128)(2,1)} %param.4), kind=kOutput, calls=%fused_computation.24 | convolution fusion | flops 8589934592 | bytes 20971520 | tf_op jit(solution)/shard_map/jat,tc->cja/dot_general | solution.py:128
  23.4 6.4 %all-to-all-start.2 = ((bf16[768,8,128]{2,1,0:T(8,128)(2,1)}), bf16[768,8,128]{2,1,0:T(8,128)(2,1)S(1)}, u32[]{:S(2)}, u32[]{:S(2)}) async-start(bf16[768,8,128]{2,1,0:T(8,128)(2,1)} %bitcast.17), calls=%async_computation.2 | async-start | bytes 3145728 | tf_op jit(solution)/shard_map/all_to_all | solution.py:151
  29.8 2.2 slice.53
  32.0 3.0 %copy.7 = bf16[4,2,2,2,40,8,128]{6,5,4,3,2,1,0:T(8,128)(2,1)S(1)} copy(bf16[4,2,2,2,40,8,128]{6,4,3,2,1,0,5:T(8,128)(2,1)S(1)} %bitcast.57) | data formatting | bytes 5242880 | tf_op jit(solution)/shard_map/reshape | solution.py:143
  37.3 14.7 %all-to-all-done.2 = bf16[768,8,128]{2,1,0:T(8,128)(2,1)S(1)} async-done(((bf16[768,8,128]{2,1,0:T(8,128)(2,1)}), bf16[768,8,128]{2,1,0:T(8,128)(2,1)S(1)}, u32[]{:S(2)}, u32[]{:S(2)}) %all-to-all-start.2) | async-done | bytes 1572896 | tf_op jit(solution)/shard_map/all_to_all | solution.py:151
  53.1 3.7 %all-to-all-start = ((bf16[1280,8,128]{2,1,0:T(8,128)(2,1)}), bf16[1280,8,128]{2,1,0:T(8,128)(2,1)S(1)}, u32[]{:S(2)}, u32[]{:S(2)}) async-start(bf16[1280,8,128]{2,1,0:T(8,128)(2,1)} %bitcast.7), calls=%async_computation | async-start | bytes 5242880 | tf_op jit(solution)/shard_map/all_to_all | solution.py:151
  56.9 3.0 %copy.24 = bf16[48,16,8,128]{3,2,1,0:T(8,128)(2,1)} copy(bf16[48,16,8,128]{3,2,0,1:T(8,128)(2,1)} %bitcast.59) | data formatting | bytes 3145728 | tf_op jit(solution)/shard_map/all_to_all | solution.py:151
  59.9 2.6 %copy.15 = bf16[48,128,128]{2,1,0:T(8,128)(2,1)} copy(bf16[48,128,128]{1,2,0:T(8,128)(2,1)} %bitcast.60) | data formatting | bytes 3145728 | tf_op jit(solution)/shard_map/transpose | solution.py:152
  62.5 3.9 %collective-permute-start.2 = (bf16[2,24,128,128]{3,2,1,0:T(8,128)(2,1)}, bf16[2,24,128,128]{3,2,1,0:T(8,128)(2,1)}, u32[]{:S(2)}, u32[]{:S(2)}) collective-permute-start(bf16[2,24,128,128]{3,2,1,0:T(8,128)(2,1)} %bitcast.62), channel_id=1, source_target_pairs={{16,0},{32,16},{48,32},{80,64},{96,80},{112,96},{17,1},{33,17},{49... | collective-permute-start | bytes 4718600 | tf_op jit(solution)/shard_map/ppermute | solution.py:153
  67.8 22.5 %all-to-all-done = bf16[1280,8,128]{2,1,0:T(8,128)(2,1)S(1)} async-done(((bf16[1280,8,128]{2,1,0:T(8,128)(2,1)}), bf16[1280,8,128]{2,1,0:T(8,128)(2,1)S(1)}, u32[]{:S(2)}, u32[]{:S(2)}) %all-to-all-start) | async-done | bytes 2621472 | tf_op jit(solution)/shard_map/all_to_all | solution.py:151
  90.3 2.2 copy.23
  92.5 3.2 %copy.10 = bf16[80,128,128]{2,1,0:T(8,128)(2,1)S(1)} copy(bf16[80,128,128]{1,2,0:T(8,128)(2,1)} %bitcast.58) | data formatting | bytes 5242880 | tf_op jit(solution)/shard_map/transpose | solution.py:152
  95.8 4.2 %collective-permute-start = (bf16[2,40,128,128]{3,2,1,0:T(8,128)(2,1)S(1)}, bf16[2,40,128,128]{3,2,1,0:T(8,128)(2,1)}, u32[]{:S(2)}, u32[]{:S(2)}) collective-permute-start(bf16[2,40,128,128]{3,2,1,0:T(8,128)(2,1)S(1)} %bitcast.52), channel_id=1, source_target_pairs={{16,0},{32,16},{48,32},{80,64},{96,80},{112,96},{17,1},{33,17},{49... | collective-permute-start | bytes 7864328 | tf_op jit(solution)/shard_map/ppermute | solution.py:153
  101.3 7.9 %collective-permute-done.3.wrap_ref = bf16[2,24,128,128]{3,2,1,0:T(8,128)(2,1)} collective-permute-done((bf16[2,24,128,128]{3,2,1,0:T(8,128)(2,1)}, bf16[2,24,128,128]{3,2,1,0:T(8,128)(2,1)}, u32[]{:S(2)}, u32[]{:S(2)}) %collective-permute-start.3) | collective-permute-done | bytes 1572896 | tf_op jit(solution)/shard_map/ppermute | solution.py:154
  109.3 13.3 %shard_map.47 = bf16[16,2,24,8,128]{4,3,2,1,0:T(8,128)(2,1)} custom-call(bf16[2,24,128,128]{3,2,1,0:T(8,128)(2,1)} %bitcast.64, bf16[2,24,128,128]{3,2,1,0:T(8,128)(2,1)} %collective-permute-done.2.next_ref, bf16[2,24,128,128]{3,2,1,0:T(8,128)(2,1)} %collective-permute-done.3.wrap_ref), custom_call_target="tpu_custom_call" | custom-call | tf_op jit(solution)/shard_map/pallas_call | solution.py:101
  122.6 4.8 %all-to-all-start.3 = ((bf16[16,2,24,8,128]{4,3,2,1,0:T(8,128)(2,1)}), bf16[16,2,24,8,128]{4,3,2,1,0:T(8,128)(2,1)}, u32[]{:S(2)}, u32[]{:S(2)}) async-start(bf16[16,2,24,8,128]{4,3,2,1,0:T(8,128)(2,1)} %shard_map.47), calls=%async_computation.3 | async-start | bytes 3145728 | tf_op jit(solution)/shard_map/all_to_all | solution.py:156
  127.3 28.4 %collective-permute-done.next_ref = bf16[2,40,128,128]{3,2,1,0:T(8,128)(2,1)} collective-permute-done((bf16[2,40,128,128]{3,2,1,0:T(8,128)(2,1)S(1)}, bf16[2,40,128,128]{3,2,1,0:T(8,128)(2,1)}, u32[]{:S(2)}, u32[]{:S(2)}) %collective-permute-start) | collective-permute-done | bytes 2621472 | tf_op jit(solution)/shard_map/ppermute | solution.py:153
  155.7 8.7 %collective-permute-done.1.wrap_ref = bf16[2,40,128,128]{3,2,1,0:T(8,128)(2,1)} collective-permute-done((bf16[2,40,128,128]{3,2,1,0:T(8,128)(2,1)S(1)}, bf16[2,40,128,128]{3,2,1,0:T(8,128)(2,1)}, u32[]{:S(2)}, u32[]{:S(2)}) %collective-permute-start.1) | collective-permute-done | bytes 2621472 | tf_op jit(solution)/shard_map/ppermute | solution.py:154
  164.5 20.7 %shard_map.46 = bf16[16,2,40,8,128]{4,3,2,1,0:T(8,128)(2,1)} custom-call(bf16[2,40,128,128]{3,2,1,0:T(8,128)(2,1)} %bitcast.54, bf16[2,40,128,128]{3,2,1,0:T(8,128)(2,1)} %collective-permute-done.next_ref, bf16[2,40,128,128]{3,2,1,0:T(8,128)(2,1)} %collective-permute-done.1.wrap_ref), custom_call_target="tpu_custom_call" | custom-call | tf_op jit(solution)/shard_map/pallas_call | solution.py:101
  185.1 4.6 %all-to-all-start.1 = ((bf16[16,2,40,8,128]{4,3,2,1,0:T(8,128)(2,1)}), bf16[16,2,40,8,128]{4,3,2,1,0:T(8,128)(2,1)S(1)}, u32[]{:S(2)}, u32[]{:S(2)}) async-start(bf16[16,2,40,8,128]{4,3,2,1,0:T(8,128)(2,1)} %shard_map.46), calls=%async_computation.1 | async-start | bytes 5242880 | tf_op jit(solution)/shard_map/all_to_all | solution.py:156
  192.0 5.5 %broadcast_select_fusion = bf16[4,2,2,2,40,2048]{5,4,3,2,1,0:T(8,128)(2,1)} fusion(bf16[4,2,2,2,40,2048]{5,4,3,2,1,0:T(8,128)(2,1)} %constant.34, bf16[4,2,2,2,40,2048]{5,4,3,2,1,0:T(8,128)(2,1)} %constant.33, pred[]{:T(512)S(6)} %lt.3), kind=kLoop, calls=%fused_computation.4 | loop fusion | flops 2621440 | bytes 15728641 | tf_op jit(solution)/shard_map/jit(_where)/select_n | solution.py:144
  197.4 7.2 %fusion.7 = f32[8,128,2048]{2,1,0:T(8,128)} fusion(bf16[768,2048,1]{1,0,2:T(8,128)(2,1)S(1)} %bitcast.51, bf16[768,8,128]{2,1,0:T(8,128)(2,1)} %bitcast.23), kind=kOutput, calls=%fused_computation.19 | convolution fusion | flops 3221225472 | bytes 13107200 | tf_op jit(solution)/shard_map/hak,hl->akl/dot_general | solution.py:159
  204.6 18.5 %all-to-all-done.1 = bf16[16,2,40,8,128]{4,3,2,1,0:T(8,128)(2,1)S(1)} async-done(((bf16[16,2,40,8,128]{4,3,2,1,0:T(8,128)(2,1)}), bf16[16,2,40,8,128]{4,3,2,1,0:T(8,128)(2,1)S(1)}, u32[]{:S(2)}, u32[]{:S(2)}) %all-to-all-start.1) | async-done | bytes 2621472 | tf_op jit(solution)/shard_map/all_to_all | solution.py:156
  223.2 11.1 %add_convert_fusion = bf16[8,128,2048]{2,1,0:T(8,128)(2,1)} fusion(f32[8,128,2048]{2,1,0:T(8,128)} %fusion.7, bf16[1280,2048,1]{1,0,2:T(8,128)(2,1)} %bitcast.46, bf16[1280,8,128]{2,1,0:T(8,128)(2,1)S(1)} %bitcast.55), kind=kOutput, calls=%fused_computation.3 | convolution fusion | flops 5372903424 | bytes 20447232 | tf_op jit(solution)/shard_map/hak,hl->akl/dot_general | solution.py:159
  (23 shorter events, 18.9 us)
Async XLA Ops:
  14.2 1.1 copy-start.3
  17.5 2.0 copy-start
  23.4 28.6 %all-to-all-start.2 = ((bf16[768,8,128]{2,1,0:T(8,128)(2,1)}), bf16[768,8,128]{2,1,0:T(8,128)(2,1)S(1)}, u32[]{:S(2)}, u32[]{:S(2)}) async-start(bf16[768,8,128]{2,1,0:T(8,128)(2,1)} %bitcast.17), calls=%async_computation.2 | async-start | bytes 3145728 | tf_op jit(solution)/shard_map/all_to_all | solution.py:151
  52.0 1.1 copy-start.2
  53.1 37.1 %all-to-all-start = ((bf16[1280,8,128]{2,1,0:T(8,128)(2,1)}), bf16[1280,8,128]{2,1,0:T(8,128)(2,1)S(1)}, u32[]{:S(2)}, u32[]{:S(2)}) async-start(bf16[1280,8,128]{2,1,0:T(8,128)(2,1)} %bitcast.7), calls=%async_computation | async-start | bytes 5242880 | tf_op jit(solution)/shard_map/all_to_all | solution.py:151
  62.5 38.8 %collective-permute-start.2 = (bf16[2,24,128,128]{3,2,1,0:T(8,128)(2,1)}, bf16[2,24,128,128]{3,2,1,0:T(8,128)(2,1)}, u32[]{:S(2)}, u32[]{:S(2)}) collective-permute-start(bf16[2,24,128,128]{3,2,1,0:T(8,128)(2,1)} %bitcast.62), channel_id=1, source_target_pairs={{16,0},{32,16},{48,32},{80,64},{96,80},{112,96},{17,1},{33,17},{49... | collective-permute-start | bytes 4718600 | tf_op jit(solution)/shard_map/ppermute | solution.py:153
  66.5 42.8 %collective-permute-start.3 = (bf16[2,24,128,128]{3,2,1,0:T(8,128)(2,1)}, bf16[2,24,128,128]{3,2,1,0:T(8,128)(2,1)}, u32[]{:S(2)}, u32[]{:S(2)}) collective-permute-start(bf16[2,24,128,128]{3,2,1,0:T(8,128)(2,1)} %bitcast.63), channel_id=1, source_target_pairs={{64,50},{65,51},{66,48},{67,49},{68,54},{69,55},{70,52},{71,53},{7... | collective-permute-start | bytes 4718600 | tf_op jit(solution)/shard_map/ppermute | solution.py:154
  95.8 26.8 %copy-start.1 = (bf16[80,128,128]{2,1,0:T(8,128)(2,1)}, bf16[80,128,128]{2,1,0:T(8,128)(2,1)S(1)}, u32[]{:S(2)}) copy-start(bf16[80,128,128]{2,1,0:T(8,128)(2,1)S(1)} %copy.10) | copy-start | bytes 7864324
  95.8 60.0 %collective-permute-start = (bf16[2,40,128,128]{3,2,1,0:T(8,128)(2,1)S(1)}, bf16[2,40,128,128]{3,2,1,0:T(8,128)(2,1)}, u32[]{:S(2)}, u32[]{:S(2)}) collective-permute-start(bf16[2,40,128,128]{3,2,1,0:T(8,128)(2,1)S(1)} %bitcast.52), channel_id=1, source_target_pairs={{16,0},{32,16},{48,32},{80,64},{96,80},{112,96},{17,1},{33,17},{49... | collective-permute-start | bytes 7864328 | tf_op jit(solution)/shard_map/ppermute | solution.py:153
  100.0 64.5 %collective-permute-start.1 = (bf16[2,40,128,128]{3,2,1,0:T(8,128)(2,1)S(1)}, bf16[2,40,128,128]{3,2,1,0:T(8,128)(2,1)}, u32[]{:S(2)}, u32[]{:S(2)}) collective-permute-start(bf16[2,40,128,128]{3,2,1,0:T(8,128)(2,1)S(1)} %bitcast.53), channel_id=1, source_target_pairs={{64,50},{65,51},{66,48},{67,49},{68,54},{69,55},{70,52},{71,53},{7... | collective-permute-start | bytes 7864328 | tf_op jit(solution)/shard_map/ppermute | solution.py:154
  122.6 62.6 %all-to-all-start.3 = ((bf16[16,2,24,8,128]{4,3,2,1,0:T(8,128)(2,1)}), bf16[16,2,24,8,128]{4,3,2,1,0:T(8,128)(2,1)}, u32[]{:S(2)}, u32[]{:S(2)}) async-start(bf16[16,2,24,8,128]{4,3,2,1,0:T(8,128)(2,1)} %shard_map.47), calls=%async_computation.3 | async-start | bytes 3145728 | tf_op jit(solution)/shard_map/all_to_all | solution.py:156
  185.1 38.0 %all-to-all-start.1 = ((bf16[16,2,40,8,128]{4,3,2,1,0:T(8,128)(2,1)}), bf16[16,2,40,8,128]{4,3,2,1,0:T(8,128)(2,1)S(1)}, u32[]{:S(2)}, u32[]{:S(2)}) async-start(bf16[16,2,40,8,128]{4,3,2,1,0:T(8,128)(2,1)} %shard_map.46), calls=%async_computation.1 | async-start | bytes 5242880 | tf_op jit(solution)/shard_map/all_to_all | solution.py:156

commit v4 on v2

--- a/solution.py
+++ b/solution.py
@@ -96,7 +96,7 @@
 
 def cross(own_t, next_t, wrap_t, parts, interpret=False):
     two, width, block, segs = own_t.shape
-    step = min(width, 8)
+    step = min(width, 16)
     spec = pl.BlockSpec((two, step, block, segs), lambda i: (0, i, 0, 0))
     return pl.pallas_call(
         cross_kernel,

time: 234 us -> 234 us (level)
  no operation moved by 1% of the time
where the time goes in v4:
time: 234 us; the launch traced here: 233 us
  waiting for transfers between devices  97.2 us (42%)
  Pallas kernels  34.6 us (15%)
  matrix products  30.7 us (13%)
  starting transfers between devices  30.2 us (13%)
  local copies, waits for them, and re-layouts  26.4 us (11%)
  other arithmetic  14.1 us (6%)
    all_to_all x2, waiting for transfers between devices, body(): own = lax.all_to_all(piece, 'tm', split_axis=0, concat_axis=1, tiled=True)  35.8 us
    pallas_call x2, Pallas kernels, cross(): pl.pallas_call(cross_kernel, grid=(width // step,), in_specs=[spec, spec,...  34.6 us
    ppermute x2, waiting for transfers between devices, body(): next_t = lax.ppermute(own_t, 'chan', inner_route)  31.3 us
    dot_general x2, matrix products, body(): jnp.einsum('hak,hl->akl', gathered, rows, preferred_element_type=jnp.floa...  18.1 us
    ppermute x2, waiting for transfers between devices, body(): wrap_t = lax.ppermute(own_t, ('chan', 'tm'), wrap_route)  17.9 us
    dot_general x1, matrix products, body(): jnp.einsum('jat,tc->cja', traces, table, preferred_element_type=jnp.float32)  12.5 us
    all_to_all x2, waiting for transfers between devices, body(): lax.all_to_all(stack, 'tm', split_axis=0, concat_axis=0, tiled=True)  12.2 us
    all_to_all x2, starting transfers between devices, body(): own = lax.all_to_all(piece, 'tm', split_axis=0, concat_axis=1, tiled=True)  10.2 us
  transfers between devices with their start and end apart: 8, of which 7 were waited for; matrix products, arithmetic and copies ran while one was open for 14% of the time, Pallas kernels for 15%

profile of v4, /device:TPU:6, one launch (start us, length us, event | category | flops | bytes accessed | tf_op | source)
XLA Modules:
  0.0 233.3 jit_solution(2509854003569546951)
XLA Ops:
  0.0 12.5 %fusion.12 = f32[2048,8,128]{2,0,1:T(8,128)S(1)} fusion(bf16[2048,2048,1]{0,1,2:T(8,128)(2,1)} %constant.38, bf16[8,128,2048]{2,1,0:T(8,128)(2,1)} %param.4), kind=kOutput, calls=%fused_computation.25 | convolution fusion | flops 8589934592 | bytes 20971520 | tf_op jit(solution)/shard_map/jat,tc->cja/dot_general | solution.py:128
  19.8 3.3 %copy.12 = bf16[4,2,2,2,32,8,128]{6,5,4,3,2,1,0:T(8,128)(2,1)S(1)} copy(bf16[4,2,2,2,32,8,128]{6,4,3,2,1,0,5:T(8,128)(2,1)S(1)} %bitcast.63) | data formatting | bytes 4194304 | tf_op jit(solution)/shard_map/reshape;squeeze | solution.py:143
  25.1 6.4 %all-to-all-start.2 = ((bf16[1024,8,128]{2,1,0:T(8,128)(2,1)}), bf16[1024,8,128]{2,1,0:T(8,128)(2,1)S(1)}, u32[]{:S(2)}, u32[]{:S(2)}) async-start(bf16[1024,8,128]{2,1,0:T(8,128)(2,1)} %bitcast.53), calls=%async_computation.2 | async-start | bytes 4194304 | tf_op jit(solution)/shard_map/all_to_all | solution.py:149
  31.5 4.9 %copy.7 = bf16[4,2,2,2,32,8,128]{6,5,4,3,2,1,0:T(8,128)(2,1)S(1)} copy(bf16[4,2,2,2,32,8,128]{6,4,3,2,1,0,5:T(8,128)(2,1)} %bitcast.62) | data formatting | bytes 4194304 | tf_op jit(solution)/shard_map/reshape;squeeze | solution.py:143
  38.3 21.0 %all-to-all-done.2 = bf16[1024,8,128]{2,1,0:T(8,128)(2,1)S(1)} async-done(((bf16[1024,8,128]{2,1,0:T(8,128)(2,1)}), bf16[1024,8,128]{2,1,0:T(8,128)(2,1)S(1)}, u32[]{:S(2)}, u32[]{:S(2)}) %all-to-all-start.2) | async-done | bytes 2097184 | tf_op jit(solution)/shard_map/all_to_all | solution.py:149
  60.6 3.7 %all-to-all-start = ((bf16[1024,8,128]{2,1,0:T(8,128)(2,1)}), bf16[1024,8,128]{2,1,0:T(8,128)(2,1)S(1)}, u32[]{:S(2)}, u32[]{:S(2)}) async-start(bf16[1024,8,128]{2,1,0:T(8,128)(2,1)} %bitcast.7), calls=%async_computation | async-start | bytes 4194304 | tf_op jit(solution)/shard_map/all_to_all | solution.py:149
  64.4 3.5 %copy.23 = bf16[64,16,8,128]{3,2,1,0:T(8,128)(2,1)} copy(bf16[64,16,8,128]{3,2,0,1:T(8,128)(2,1)} %bitcast.52) | data formatting | bytes 4194304 | tf_op jit(solution)/shard_map/all_to_all | solution.py:149
  67.9 4.1 %copy.15 = bf16[64,128,128]{2,1,0:T(8,128)(2,1)} copy(bf16[64,128,128]{1,2,0:T(8,128)(2,1)} %bitcast.54) | data formatting | bytes 4194304 | tf_op jit(solution)/shard_map/transpose | solution.py:150
  71.9 4.1 %collective-permute-start.2 = (bf16[2,32,128,128]{3,2,1,0:T(8,128)(2,1)}, bf16[2,32,128,128]{3,2,1,0:T(8,128)(2,1)}, u32[]{:S(2)}, u32[]{:S(2)}) collective-permute-start(bf16[2,32,128,128]{3,2,1,0:T(8,128)(2,1)} %bitcast.56), channel_id=1, source_target_pairs={{16,0},{32,16},{48,32},{80,64},{96,80},{112,96},{17,1},{33,17},{49... | collective-permute-start | bytes 6291464 | tf_op jit(solution)/shard_map/ppermute | solution.py:151
  77.3 14.9 %all-to-all-done = bf16[1024,8,128]{2,1,0:T(8,128)(2,1)S(1)} async-done(((bf16[1024,8,128]{2,1,0:T(8,128)(2,1)}), bf16[1024,8,128]{2,1,0:T(8,128)(2,1)S(1)}, u32[]{:S(2)}, u32[]{:S(2)}) %all-to-all-start) | async-done | bytes 2097184 | tf_op jit(solution)/shard_map/all_to_all | solution.py:149
  94.1 3.2 %copy.10 = bf16[64,128,128]{2,1,0:T(8,128)(2,1)S(1)} copy(bf16[64,128,128]{1,2,0:T(8,128)(2,1)} %bitcast.55) | data formatting | bytes 4194304 | tf_op jit(solution)/shard_map/transpose | solution.py:150
  97.3 4.1 %collective-permute-start = (bf16[2,32,128,128]{3,2,1,0:T(8,128)(2,1)S(1)}, bf16[2,32,128,128]{3,2,1,0:T(8,128)(2,1)}, u32[]{:S(2)}, u32[]{:S(2)}) collective-permute-start(bf16[2,32,128,128]{3,2,1,0:T(8,128)(2,1)S(1)} %bitcast.59), channel_id=1, source_target_pairs={{16,0},{32,16},{48,32},{80,64},{96,80},{112,96},{17,1},{33,17},{49... | collective-permute-start | bytes 6291464 | tf_op jit(solution)/shard_map/ppermute | solution.py:151
  102.7 18.3 %collective-permute-done.2.next_ref = bf16[2,32,128,128]{3,2,1,0:T(8,128)(2,1)} collective-permute-done((bf16[2,32,128,128]{3,2,1,0:T(8,128)(2,1)}, bf16[2,32,128,128]{3,2,1,0:T(8,128)(2,1)}, u32[]{:S(2)}, u32[]{:S(2)}) %collective-permute-start.2) | collective-permute-done | bytes 2097184 | tf_op jit(solution)/shard_map/ppermute | solution.py:151
  121.0 9.0 %collective-permute-done.3.wrap_ref = bf16[2,32,128,128]{3,2,1,0:T(8,128)(2,1)} collective-permute-done((bf16[2,32,128,128]{3,2,1,0:T(8,128)(2,1)}, bf16[2,32,128,128]{3,2,1,0:T(8,128)(2,1)}, u32[]{:S(2)}, u32[]{:S(2)}) %collective-permute-start.3) | collective-permute-done | bytes 2097184 | tf_op jit(solution)/shard_map/ppermute | solution.py:152
  130.0 17.3 %shard_map.47 = bf16[16,2,32,8,128]{4,3,2,1,0:T(8,128)(2,1)} custom-call(bf16[2,32,128,128]{3,2,1,0:T(8,128)(2,1)} %bitcast.58, bf16[2,32,128,128]{3,2,1,0:T(8,128)(2,1)} %collective-permute-done.2.next_ref, bf16[2,32,128,128]{3,2,1,0:T(8,128)(2,1)} %collective-permute-done.3.wrap_ref), custom_call_target="tpu_custom_call" | custom-call | tf_op jit(solution)/shard_map/pallas_call | solution.py:101
  147.3 4.8 %all-to-all-start.3 = ((bf16[16,2,32,8,128]{4,3,2,1,0:T(8,128)(2,1)}), bf16[16,2,32,8,128]{4,3,2,1,0:T(8,128)(2,1)}, u32[]{:S(2)}, u32[]{:S(2)}) async-start(bf16[16,2,32,8,128]{4,3,2,1,0:T(8,128)(2,1)} %shard_map.47), calls=%async_computation.3 | async-start | bytes 4194304 | tf_op jit(solution)/shard_map/all_to_all | solution.py:154
  152.1 13.0 %collective-permute-done.next_ref = bf16[2,32,128,128]{3,2,1,0:T(8,128)(2,1)} collective-permute-done((bf16[2,32,128,128]{3,2,1,0:T(8,128)(2,1)S(1)}, bf16[2,32,128,128]{3,2,1,0:T(8,128)(2,1)}, u32[]{:S(2)}, u32[]{:S(2)}) %collective-permute-start) | collective-permute-done | bytes 2097184 | tf_op jit(solution)/shard_map/ppermute | solution.py:151
  165.1 8.9 %collective-permute-done.1.wrap_ref = bf16[2,32,128,128]{3,2,1,0:T(8,128)(2,1)} collective-permute-done((bf16[2,32,128,128]{3,2,1,0:T(8,128)(2,1)S(1)}, bf16[2,32,128,128]{3,2,1,0:T(8,128)(2,1)}, u32[]{:S(2)}, u32[]{:S(2)}) %collective-permute-start.1) | collective-permute-done | bytes 2097184 | tf_op jit(solution)/shard_map/ppermute | solution.py:152
  174.0 17.3 %shard_map.46 = bf16[16,2,32,8,128]{4,3,2,1,0:T(8,128)(2,1)} custom-call(bf16[2,32,128,128]{3,2,1,0:T(8,128)(2,1)} %bitcast.61, bf16[2,32,128,128]{3,2,1,0:T(8,128)(2,1)} %collective-permute-done.next_ref, bf16[2,32,128,128]{3,2,1,0:T(8,128)(2,1)} %collective-permute-done.1.wrap_ref), custom_call_target="tpu_custom_call" | custom-call | tf_op jit(solution)/shard_map/pallas_call | solution.py:101
  191.3 4.6 %all-to-all-start.1 = ((bf16[16,2,32,8,128]{4,3,2,1,0:T(8,128)(2,1)}), bf16[16,2,32,8,128]{4,3,2,1,0:T(8,128)(2,1)S(1)}, u32[]{:S(2)}, u32[]{:S(2)}) async-start(bf16[16,2,32,8,128]{4,3,2,1,0:T(8,128)(2,1)} %shard_map.46), calls=%async_computation.1 | async-start | bytes 4194304 | tf_op jit(solution)/shard_map/all_to_all | solution.py:154
  195.9 2.8 %broadcast_select_fusion = bf16[4,2,2,2,32,2048]{5,4,3,2,1,0:T(8,128)(2,1)S(1)} fusion(bf16[4,2,2,2,32,2048]{5,4,3,2,1,0:T(8,128)(2,1)} %constant.37, bf16[4,2,2,2,32,2048]{5,4,3,2,1,0:T(8,128)(2,1)} %constant.36, pred[]{:T(512)S(6)} %lt.3), kind=kLoop, calls=%fused_computation.13 | loop fusion | flops 2097152 | bytes 12582913 | tf_op jit(solution)/shard_map/jit(_where)/select_n | solution.py:144
  203.0 8.5 %fusion.6 = f32[8,128,2048]{2,1,0:T(8,128)} fusion(bf16[1024,2048,1]{1,0,2:T(8,128)(2,1)S(1)} %bitcast.64, bf16[1024,8,128]{2,1,0:T(8,128)(2,1)} %bitcast.23), kind=kOutput, calls=%fused_computation.17 | convolution fusion | flops 4294967296 | bytes 14680064 | tf_op jit(solution)/shard_map/hak,hl->akl/dot_general | solution.py:157
  211.5 12.2 %all-to-all-done.1 = bf16[16,2,32,8,128]{4,3,2,1,0:T(8,128)(2,1)S(1)} async-done(((bf16[16,2,32,8,128]{4,3,2,1,0:T(8,128)(2,1)}), bf16[16,2,32,8,128]{4,3,2,1,0:T(8,128)(2,1)S(1)}, u32[]{:S(2)}, u32[]{:S(2)}) %all-to-all-start.1) | async-done | bytes 2097184 | tf_op jit(solution)/shard_map/all_to_all | solution.py:154
  223.7 9.6 %add_convert_fusion = bf16[8,128,2048]{2,1,0:T(8,128)(2,1)} fusion(f32[8,128,2048]{2,1,0:T(8,128)} %fusion.6, bf16[1024,2048,1]{1,0,2:T(8,128)(2,1)} %bitcast.49, bf16[1024,8,128]{2,1,0:T(8,128)(2,1)S(1)} %bitcast.50), kind=kOutput, calls=%fused_computation.3 | convolution fusion | flops 4299161600 | bytes 18874368 | tf_op jit(solution)/shard_map/hak,hl->akl/dot_general | solution.py:157
  (24 shorter events, 21.2 us)
Async XLA Ops:
  14.2 1.1 copy-start.4
  25.1 34.3 %all-to-all-start.2 = ((bf16[1024,8,128]{2,1,0:T(8,128)(2,1)}), bf16[1024,8,128]{2,1,0:T(8,128)(2,1)S(1)}, u32[]{:S(2)}, u32[]{:S(2)}) async-start(bf16[1024,8,128]{2,1,0:T(8,128)(2,1)} %bitcast.53), calls=%async_computation.2 | async-start | bytes 4194304 | tf_op jit(solution)/shard_map/all_to_all | solution.py:149
  59.3 1.3 copy-start
  60.6 31.5 %all-to-all-start = ((bf16[1024,8,128]{2,1,0:T(8,128)(2,1)}), bf16[1024,8,128]{2,1,0:T(8,128)(2,1)S(1)}, u32[]{:S(2)}, u32[]{:S(2)}) async-start(bf16[1024,8,128]{2,1,0:T(8,128)(2,1)} %bitcast.7), calls=%async_computation | async-start | bytes 4194304 | tf_op jit(solution)/shard_map/all_to_all | solution.py:149
  71.9 49.0 %collective-permute-start.2 = (bf16[2,32,128,128]{3,2,1,0:T(8,128)(2,1)}, bf16[2,32,128,128]{3,2,1,0:T(8,128)(2,1)}, u32[]{:S(2)}, u32[]{:S(2)}) collective-permute-start(bf16[2,32,128,128]{3,2,1,0:T(8,128)(2,1)} %bitcast.56), channel_id=1, source_target_pairs={{16,0},{32,16},{48,32},{80,64},{96,80},{112,96},{17,1},{33,17},{49... | collective-permute-start | bytes 6291464 | tf_op jit(solution)/shard_map/ppermute | solution.py:151
  76.0 54.0 %collective-permute-start.3 = (bf16[2,32,128,128]{3,2,1,0:T(8,128)(2,1)}, bf16[2,32,128,128]{3,2,1,0:T(8,128)(2,1)}, u32[]{:S(2)}, u32[]{:S(2)}) collective-permute-start(bf16[2,32,128,128]{3,2,1,0:T(8,128)(2,1)} %bitcast.57), channel_id=1, source_target_pairs={{64,50},{65,51},{66,48},{67,49},{68,54},{69,55},{70,52},{71,53},{7... | collective-permute-start | bytes 6291464 | tf_op jit(solution)/shard_map/ppermute | solution.py:152
  97.3 50.0 %copy-start.1 = (bf16[64,128,128]{2,1,0:T(8,128)(2,1)}, bf16[64,128,128]{2,1,0:T(8,128)(2,1)S(1)}, u32[]{:S(2)}) copy-start(bf16[64,128,128]{2,1,0:T(8,128)(2,1)S(1)} %copy.10) | copy-start | bytes 6291460
  97.3 67.8 %collective-permute-start = (bf16[2,32,128,128]{3,2,1,0:T(8,128)(2,1)S(1)}, bf16[2,32,128,128]{3,2,1,0:T(8,128)(2,1)}, u32[]{:S(2)}, u32[]{:S(2)}) collective-permute-start(bf16[2,32,128,128]{3,2,1,0:T(8,128)(2,1)S(1)} %bitcast.59), channel_id=1, source_target_pairs={{16,0},{32,16},{48,32},{80,64},{96,80},{112,96},{17,1},{33,17},{49... | collective-permute-start | bytes 6291464 | tf_op jit(solution)/shard_map/ppermute | solution.py:151
  101.4 72.6 %collective-permute-start.1 = (bf16[2,32,128,128]{3,2,1,0:T(8,128)(2,1)S(1)}, bf16[2,32,128,128]{3,2,1,0:T(8,128)(2,1)}, u32[]{:S(2)}, u32[]{:S(2)}) collective-permute-start(bf16[2,32,128,128]{3,2,1,0:T(8,128)(2,1)S(1)} %bitcast.60), channel_id=1, source_target_pairs={{64,50},{65,51},{66,48},{67,49},{68,54},{69,55},{70,52},{71,53},{7... | collective-permute-start | bytes 6291464 | tf_op jit(solution)/shard_map/ppermute | solution.py:152
  147.3 43.9 %all-to-all-start.3 = ((bf16[16,2,32,8,128]{4,3,2,1,0:T(8,128)(2,1)}), bf16[16,2,32,8,128]{4,3,2,1,0:T(8,128)(2,1)}, u32[]{:S(2)}, u32[]{:S(2)}) async-start(bf16[16,2,32,8,128]{4,3,2,1,0:T(8,128)(2,1)} %shard_map.47), calls=%async_computation.3 | async-start | bytes 4194304 | tf_op jit(solution)/shard_map/all_to_all | solution.py:154
  191.3 32.4 %all-to-all-start.1 = ((bf16[16,2,32,8,128]{4,3,2,1,0:T(8,128)(2,1)}), bf16[16,2,32,8,128]{4,3,2,1,0:T(8,128)(2,1)S(1)}, u32[]{:S(2)}, u32[]{:S(2)}) async-start(bf16[16,2,32,8,128]{4,3,2,1,0:T(8,128)(2,1)} %shard_map.46), calls=%async_computation.1 | async-start | bytes 4194304 | tf_op jit(solution)/shard_map/all_to_all | solution.py:154
  195.9 3.5 %copy-start.2 = (bf16[4,2,2,2,32,2048]{5,4,3,2,1,0:T(8,128)(2,1)S(1)}, bf16[4,2,2,2,32,2048]{5,4,3,2,1,0:T(8,128)(2,1)}, u32[]{:S(2)}) copy-start(bf16[4,2,2,2,32,2048]{5,4,3,2,1,0:T(8,128)(2,1)} %constant.33) | copy-start | bytes 12582916
  195.9 4.7 %copy-start.3 = (bf16[4,2,2,2,32,2048]{5,4,3,2,1,0:T(8,128)(2,1)S(1)}, bf16[4,2,2,2,32,2048]{5,4,3,2,1,0:T(8,128)(2,1)}, u32[]{:S(2)}) copy-start(bf16[4,2,2,2,32,2048]{5,4,3,2,1,0:T(8,128)(2,1)} %constant.34) | copy-start | bytes 12582916

commit v5 on v2

--- a/solution.py
+++ b/solution.py
@@ -72,14 +72,14 @@
         return jnp.dot(flip, x, preferred_element_type=jnp.float32).astype(jnp.bfloat16)
 
     for f in range(own_ref.shape[1]):
-        own_real = own_ref[0, f]
-        own_imag = own_ref[1, f]
+        own_real = own_ref[0, f].T
+        own_imag = own_ref[1, f].T
         own_both = jnp.concatenate([own_real, own_imag], axis=1)
         lhs = jnp.concatenate(
             [own_both, jnp.concatenate([own_imag, -own_real], axis=1)], axis=0
         )
         next_both = jnp.concatenate(
-            [next_ref[0, f] + wrap_ref[0, f], next_ref[1, f] + wrap_ref[1, f]], axis=1
+            [(next_ref[0, f] + wrap_ref[0, f]).T, (next_ref[1, f] + wrap_ref[1, f]).T], axis=1
         )
         rhs = jnp.concatenate([reverse_rows(next_both), reverse_rows(own_both)], axis=0)
         both = lax.dot_general(
@@ -147,7 +147,7 @@
     for chunk in range(CHUNKS):
         piece = swap_pairs(white[:, :, chunk]).reshape(groups * 2 * width, seg_dev, block)
         own = lax.all_to_all(piece, "tm", split_axis=0, concat_axis=1, tiled=True)
-        own_t = jnp.swapaxes(own, 1, 2).reshape(2, width, block, segments)
+        own_t = own.reshape(2, width, segments, block)
         next_t = lax.ppermute(own_t, "chan", inner_route)
         wrap_t = lax.ppermute(own_t, ("chan", "tm"), wrap_route)
         stack = cross(own_t, next_t, wrap_t, groups)

time: 234 us -> 228 us (0.974)
  local copies, waits for them, and re-layouts: 26.4 us -> 16.4 us
  waiting for transfers between devices: 97.5 us -> 99.9 us
    transpose x2 -> x0, local copies, waits for them, and re-layouts: 7.28 us -> none  [body(): own_t = jnp.swapaxes(own, 1, 2).reshape(2, width, block, segments)]
    all_to_all x2, waiting for transfers between devices: 35.8 us -> 41.5 us  [body(): own = lax.all_to_all(piece, 'tm', split_axis=0, concat_axis=1, tiled=True)]
    ppermute x2, waiting for transfers between devices: 31.6 us -> 28.2 us  [body(): next_t = lax.ppermute(own_t, 'chan', inner_route)]
  transfers between devices with their start and end apart: 8 -> 8, of which waited for: 7 -> 7; matrix products, arithmetic and copies ran while one was open for 14% -> 11% of each run, Pallas kernels for 15% -> 16%
where the time goes in v5:
time: 228 us; the launch traced here: 227 us
  waiting for transfers between devices  99.9 us (44%)
  Pallas kernels  35.2 us (15%)
  starting transfers between devices  30.9 us (14%)
  matrix products  30.6 us (13%)
  local copies, waits for them, and re-layouts  16.4 us (7%)
  other arithmetic  14 us (6%)
    all_to_all x2, waiting for transfers between devices, body(): own = lax.all_to_all(piece, 'tm', split_axis=0, concat_axis=1, tiled=True)  41.5 us
    pallas_call x2, Pallas kernels, cross(): pl.pallas_call(cross_kernel, grid=(width // step,), in_specs=[spec, spec,...  35.2 us
    ppermute x2, waiting for transfers between devices, body(): next_t = lax.ppermute(own_t, 'chan', inner_route)  28.2 us
    dot_general x2, matrix products, body(): jnp.einsum('hak,hl->akl', gathered, rows, preferred_element_type=jnp.floa...  18 us
    ppermute x2, waiting for transfers between devices, body(): wrap_t = lax.ppermute(own_t, ('chan', 'tm'), wrap_route)  17.9 us
    dot_general x1, matrix products, body(): jnp.einsum('jat,tc->cja', traces, table, preferred_element_type=jnp.float32)  12.5 us
    all_to_all x2, waiting for transfers between devices, body(): lax.all_to_all(stack, 'tm', split_axis=0, concat_axis=0, tiled=True)  12.3 us
    all_to_all x2, starting transfers between devices, body(): own = lax.all_to_all(piece, 'tm', split_axis=0, concat_axis=1, tiled=True)  10.9 us
  transfers between devices with their start and end apart: 8, of which 7 were waited for; matrix products, arithmetic and copies ran while one was open for 11% of the time, Pallas kernels for 16%

profile of v5, /device:TPU:6, one launch (start us, length us, event | category | flops | bytes accessed | tf_op | source)
XLA Modules:
  0.0 227.3 jit_solution(14059576203203300235)
XLA Ops:
  0.0 12.5 %fusion.12 = f32[2048,8,128]{2,0,1:T(8,128)S(1)} fusion(bf16[2048,2048,1]{0,1,2:T(8,128)(2,1)} %constant.38, bf16[8,128,2048]{2,1,0:T(8,128)(2,1)} %param.4), kind=kOutput, calls=%fused_computation.23 | convolution fusion | flops 8589934592 | bytes 20971520 | tf_op jit(solution)/shard_map/jat,tc->cja/dot_general | solution.py:128
  17.7 2.2 fusion.11
  19.8 3.3 %copy.11 = bf16[4,2,2,2,32,8,128]{6,5,4,3,2,1,0:T(8,128)(2,1)S(1)} copy(bf16[4,2,2,2,32,8,128]{6,4,3,2,1,0,5:T(8,128)(2,1)S(1)} %bitcast.47) | data formatting | bytes 4194304 | tf_op jit(solution)/shard_map/reshape;squeeze | solution.py:143
  25.1 6.4 %all-to-all-start.2 = ((bf16[1024,8,128]{2,1,0:T(8,128)(2,1)}), bf16[1024,8,128]{2,1,0:T(8,128)(2,1)S(1)}, u32[]{:S(2)}, u32[]{:S(2)}) async-start(bf16[1024,8,128]{2,1,0:T(8,128)(2,1)} %bitcast.42), calls=%async_computation.2 | async-start | bytes 4194304 | tf_op jit(solution)/shard_map/all_to_all | solution.py:149
  31.5 4.9 %copy.7 = bf16[4,2,2,2,32,8,128]{6,5,4,3,2,1,0:T(8,128)(2,1)S(1)} copy(bf16[4,2,2,2,32,8,128]{6,4,3,2,1,0,5:T(8,128)(2,1)} %bitcast.46) | data formatting | bytes 4194304 | tf_op jit(solution)/shard_map/reshape;squeeze | solution.py:143
  38.3 21.0 %all-to-all-done.2 = bf16[1024,8,128]{2,1,0:T(8,128)(2,1)S(1)} async-done(((bf16[1024,8,128]{2,1,0:T(8,128)(2,1)}), bf16[1024,8,128]{2,1,0:T(8,128)(2,1)S(1)}, u32[]{:S(2)}, u32[]{:S(2)}) %all-to-all-start.2) | async-done | bytes 2097184 | tf_op jit(solution)/shard_map/all_to_all | solution.py:149
  59.3 4.4 %all-to-all-start = ((bf16[1024,8,128]{2,1,0:T(8,128)(2,1)}), bf16[1024,8,128]{2,1,0:T(8,128)(2,1)}, u32[]{:S(2)}, u32[]{:S(2)}) async-start(bf16[1024,8,128]{2,1,0:T(8,128)(2,1)} %bitcast.7), calls=%async_computation | async-start | bytes 4194304 | tf_op jit(solution)/shard_map/all_to_all | solution.py:149
  65.7 4.1 %collective-permute-start.2 = (bf16[2,32,128,128]{3,2,1,0:T(8,128)(2,1)}, bf16[2,32,128,128]{3,2,1,0:T(8,128)(2,1)}, u32[]{:S(2)}, u32[]{:S(2)}) collective-permute-start(bf16[2,32,128,128]{3,2,1,0:T(8,128)(2,1)} %bitcast.18.own_ref), channel_id=1, source_target_pairs={{16,0},{32,16},{48,32},{80,64},{96,80},{112,96},{17,1},{33,17},{49... | collective-permute-start | bytes 6291464 | tf_op jit(solution)/shard_map/ppermute | solution.py:151
  71.0 20.6 %all-to-all-done = bf16[1024,8,128]{2,1,0:T(8,128)(2,1)} async-done(((bf16[1024,8,128]{2,1,0:T(8,128)(2,1)}), bf16[1024,8,128]{2,1,0:T(8,128)(2,1)}, u32[]{:S(2)}, u32[]{:S(2)}) %all-to-all-start) | async-done | bytes 2097184 | tf_op jit(solution)/shard_map/all_to_all | solution.py:149
  91.6 2.2 copy.9
  93.8 4.1 %collective-permute-start = (bf16[2,32,128,128]{3,2,1,0:T(8,128)(2,1)S(1)}, bf16[2,32,128,128]{3,2,1,0:T(8,128)(2,1)}, u32[]{:S(2)}, u32[]{:S(2)}) collective-permute-start(bf16[2,32,128,128]{3,2,1,0:T(8,128)(2,1)S(1)} %bitcast.43), channel_id=1, source_target_pairs={{16,0},{32,16},{48,32},{80,64},{96,80},{112,96},{17,1},{33,17},{49... | collective-permute-start | bytes 6291464 | tf_op jit(solution)/shard_map/ppermute | solution.py:151
  99.2 15.5 %collective-permute-done.2.next_ref = bf16[2,32,128,128]{3,2,1,0:T(8,128)(2,1)} collective-permute-done((bf16[2,32,128,128]{3,2,1,0:T(8,128)(2,1)}, bf16[2,32,128,128]{3,2,1,0:T(8,128)(2,1)}, u32[]{:S(2)}, u32[]{:S(2)}) %collective-permute-start.2) | collective-permute-done | bytes 2097184 | tf_op jit(solution)/shard_map/ppermute | solution.py:151
  114.7 9.0 %collective-permute-done.3.wrap_ref = bf16[2,32,128,128]{3,2,1,0:T(8,128)(2,1)} collective-permute-done((bf16[2,32,128,128]{3,2,1,0:T(8,128)(2,1)}, bf16[2,32,128,128]{3,2,1,0:T(8,128)(2,1)}, u32[]{:S(2)}, u32[]{:S(2)}) %collective-permute-start.3) | collective-permute-done | bytes 2097184 | tf_op jit(solution)/shard_map/ppermute | solution.py:152
  123.8 17.6 %shard_map.47 = bf16[16,2,32,8,128]{4,3,2,1,0:T(8,128)(2,1)} custom-call(bf16[2,32,128,128]{3,2,1,0:T(8,128)(2,1)} %bitcast.18.own_ref, bf16[2,32,128,128]{3,2,1,0:T(8,128)(2,1)} %collective-permute-done.2.next_ref, bf16[2,32,128,128]{3,2,1,0:T(8,128)(2,1)} %collective-permute-done.3.wrap_ref), custom_call_target="tpu_custom_call" | custom-call | tf_op jit(solution)/shard_map/pallas_call | solution.py:101
  141.4 4.7 %all-to-all-start.3 = ((bf16[16,2,32,8,128]{4,3,2,1,0:T(8,128)(2,1)}), bf16[16,2,32,8,128]{4,3,2,1,0:T(8,128)(2,1)}, u32[]{:S(2)}, u32[]{:S(2)}) async-start(bf16[16,2,32,8,128]{4,3,2,1,0:T(8,128)(2,1)} %shard_map.47), calls=%async_computation.3 | async-start | bytes 4194304 | tf_op jit(solution)/shard_map/all_to_all | solution.py:154
  146.2 12.7 %collective-permute-done.next_ref = bf16[2,32,128,128]{3,2,1,0:T(8,128)(2,1)} collective-permute-done((bf16[2,32,128,128]{3,2,1,0:T(8,128)(2,1)S(1)}, bf16[2,32,128,128]{3,2,1,0:T(8,128)(2,1)}, u32[]{:S(2)}, u32[]{:S(2)}) %collective-permute-start) | collective-permute-done | bytes 2097184 | tf_op jit(solution)/shard_map/ppermute | solution.py:151
  158.8 8.9 %collective-permute-done.1.wrap_ref = bf16[2,32,128,128]{3,2,1,0:T(8,128)(2,1)} collective-permute-done((bf16[2,32,128,128]{3,2,1,0:T(8,128)(2,1)S(1)}, bf16[2,32,128,128]{3,2,1,0:T(8,128)(2,1)}, u32[]{:S(2)}, u32[]{:S(2)}) %collective-permute-start.1) | collective-permute-done | bytes 2097184 | tf_op jit(solution)/shard_map/ppermute | solution.py:152
  167.7 17.6 %shard_map.46 = bf16[16,2,32,8,128]{4,3,2,1,0:T(8,128)(2,1)} custom-call(bf16[2,32,128,128]{3,2,1,0:T(8,128)(2,1)} %bitcast.45, bf16[2,32,128,128]{3,2,1,0:T(8,128)(2,1)} %collective-permute-done.next_ref, bf16[2,32,128,128]{3,2,1,0:T(8,128)(2,1)} %collective-permute-done.1.wrap_ref), custom_call_target="tpu_custom_call" | custom-call | tf_op jit(solution)/shard_map/pallas_call | solution.py:101
  185.3 4.6 %all-to-all-start.1 = ((bf16[16,2,32,8,128]{4,3,2,1,0:T(8,128)(2,1)}), bf16[16,2,32,8,128]{4,3,2,1,0:T(8,128)(2,1)S(1)}, u32[]{:S(2)}, u32[]{:S(2)}) async-start(bf16[16,2,32,8,128]{4,3,2,1,0:T(8,128)(2,1)} %shard_map.46), calls=%async_computation.1 | async-start | bytes 4194304 | tf_op jit(solution)/shard_map/all_to_all | solution.py:154
  189.9 2.8 %broadcast_select_fusion = bf16[4,2,2,2,32,2048]{5,4,3,2,1,0:T(8,128)(2,1)S(1)} fusion(bf16[4,2,2,2,32,2048]{5,4,3,2,1,0:T(8,128)(2,1)} %constant.37, bf16[4,2,2,2,32,2048]{5,4,3,2,1,0:T(8,128)(2,1)} %constant.36, pred[]{:T(512)S(6)} %lt.3), kind=kLoop, calls=%fused_computation.13 | loop fusion | flops 2097152 | bytes 12582913 | tf_op jit(solution)/shard_map/jit(_where)/select_n | solution.py:144
  194.6 2.4 %broadcast_select_fusion.1 = bf16[4,2,2,2,32,2048]{5,4,3,2,1,0:T(8,128)(2,1)} fusion(bf16[4,2,2,2,32,2048]{5,4,3,2,1,0:T(8,128)(2,1)S(1)} %copy-done.2, bf16[4,2,2,2,32,2048]{5,4,3,2,1,0:T(8,128)(2,1)S(1)} %copy-done.1, pred[]{:T(512)S(6)} %lt.3), kind=kLoop, calls=%fused_computation.14 | loop fusion | flops 2097152 | bytes 12582913 | tf_op jit(solution)/shard_map/jit(_where)/select_n | solution.py:144
  197.0 8.4 %fusion.6 = f32[8,128,2048]{2,1,0:T(8,128)} fusion(bf16[1024,2048,1]{1,0,2:T(8,128)(2,1)S(1)} %bitcast.48, bf16[1024,8,128]{2,1,0:T(8,128)(2,1)} %bitcast.19), kind=kOutput, calls=%fused_computation.17 | convolution fusion | flops 4294967296 | bytes 14680064 | tf_op jit(solution)/shard_map/hak,hl->akl/dot_general | solution.py:157
  205.4 12.3 %all-to-all-done.1 = bf16[16,2,32,8,128]{4,3,2,1,0:T(8,128)(2,1)S(1)} async-done(((bf16[16,2,32,8,128]{4,3,2,1,0:T(8,128)(2,1)}), bf16[16,2,32,8,128]{4,3,2,1,0:T(8,128)(2,1)S(1)}, u32[]{:S(2)}, u32[]{:S(2)}) %all-to-all-start.1) | async-done | bytes 2097184 | tf_op jit(solution)/shard_map/all_to_all | solution.py:154
  217.7 9.6 %add_convert_fusion = bf16[8,128,2048]{2,1,0:T(8,128)(2,1)} fusion(f32[8,128,2048]{2,1,0:T(8,128)} %fusion.6, bf16[1024,2048,1]{1,0,2:T(8,128)(2,1)} %bitcast.39, bf16[1024,8,128]{2,1,0:T(8,128)(2,1)S(1)} %bitcast.40), kind=kOutput, calls=%fused_computation.3 | convolution fusion | flops 4299161600 | bytes 18874368 | tf_op jit(solution)/shard_map/hak,hl->akl/dot_general | solution.py:157
  (20 shorter events, 15.3 us)
Async XLA Ops:
  14.2 1.1 copy-start.3
  25.1 34.3 %all-to-all-start.2 = ((bf16[1024,8,128]{2,1,0:T(8,128)(2,1)}), bf16[1024,8,128]{2,1,0:T(8,128)(2,1)S(1)}, u32[]{:S(2)}, u32[]{:S(2)}) async-start(bf16[1024,8,128]{2,1,0:T(8,128)(2,1)} %bitcast.42), calls=%async_computation.2 | async-start | bytes 4194304 | tf_op jit(solution)/shard_map/all_to_all | solution.py:149
  59.3 32.3 %all-to-all-start = ((bf16[1024,8,128]{2,1,0:T(8,128)(2,1)}), bf16[1024,8,128]{2,1,0:T(8,128)(2,1)}, u32[]{:S(2)}, u32[]{:S(2)}) async-start(bf16[1024,8,128]{2,1,0:T(8,128)(2,1)} %bitcast.7), calls=%async_computation | async-start | bytes 4194304 | tf_op jit(solution)/shard_map/all_to_all | solution.py:149
  65.7 49.1 %collective-permute-start.2 = (bf16[2,32,128,128]{3,2,1,0:T(8,128)(2,1)}, bf16[2,32,128,128]{3,2,1,0:T(8,128)(2,1)}, u32[]{:S(2)}, u32[]{:S(2)}) collective-permute-start(bf16[2,32,128,128]{3,2,1,0:T(8,128)(2,1)} %bitcast.18.own_ref), channel_id=1, source_target_pairs={{16,0},{32,16},{48,32},{80,64},{96,80},{112,96},{17,1},{33,17},{49... | collective-permute-start | bytes 6291464 | tf_op jit(solution)/shard_map/ppermute | solution.py:151
  69.7 54.0 %collective-permute-start.3 = (bf16[2,32,128,128]{3,2,1,0:T(8,128)(2,1)}, bf16[2,32,128,128]{3,2,1,0:T(8,128)(2,1)}, u32[]{:S(2)}, u32[]{:S(2)}) collective-permute-start(bf16[2,32,128,128]{3,2,1,0:T(8,128)(2,1)} %bitcast.18.own_ref), channel_id=1, source_target_pairs={{64,50},{65,51},{66,48},{67,49},{68,54},{69,55},{70,52},{71,53},{7... | collective-permute-start | bytes 6291464 | tf_op jit(solution)/shard_map/ppermute | solution.py:152
  93.8 47.6 %copy-start = (bf16[64,16,8,128]{3,2,1,0:T(8,128)(2,1)}, bf16[64,16,8,128]{3,2,1,0:T(8,128)(2,1)S(1)}, u32[]{:S(2)}) copy-start(bf16[64,16,8,128]{3,2,1,0:T(8,128)(2,1)S(1)} %copy.9) | copy-start | bytes 6291460
  93.8 65.0 %collective-permute-start = (bf16[2,32,128,128]{3,2,1,0:T(8,128)(2,1)S(1)}, bf16[2,32,128,128]{3,2,1,0:T(8,128)(2,1)}, u32[]{:S(2)}, u32[]{:S(2)}) collective-permute-start(bf16[2,32,128,128]{3,2,1,0:T(8,128)(2,1)S(1)} %bitcast.43), channel_id=1, source_target_pairs={{16,0},{32,16},{48,32},{80,64},{96,80},{112,96},{17,1},{33,17},{49... | collective-permute-start | bytes 6291464 | tf_op jit(solution)/shard_map/ppermute | solution.py:151
  97.9 69.8 %collective-permute-start.1 = (bf16[2,32,128,128]{3,2,1,0:T(8,128)(2,1)S(1)}, bf16[2,32,128,128]{3,2,1,0:T(8,128)(2,1)}, u32[]{:S(2)}, u32[]{:S(2)}) collective-permute-start(bf16[2,32,128,128]{3,2,1,0:T(8,128)(2,1)S(1)} %bitcast.44), channel_id=1, source_target_pairs={{64,50},{65,51},{66,48},{67,49},{68,54},{69,55},{70,52},{71,53},{7... | collective-permute-start | bytes 6291464 | tf_op jit(solution)/shard_map/ppermute | solution.py:152
  141.4 43.9 %all-to-all-start.3 = ((bf16[16,2,32,8,128]{4,3,2,1,0:T(8,128)(2,1)}), bf16[16,2,32,8,128]{4,3,2,1,0:T(8,128)(2,1)}, u32[]{:S(2)}, u32[]{:S(2)}) async-start(bf16[16,2,32,8,128]{4,3,2,1,0:T(8,128)(2,1)} %shard_map.47), calls=%async_computation.3 | async-start | bytes 4194304 | tf_op jit(solution)/shard_map/all_to_all | solution.py:154
  185.3 32.4 %all-to-all-start.1 = ((bf16[16,2,32,8,128]{4,3,2,1,0:T(8,128)(2,1)}), bf16[16,2,32,8,128]{4,3,2,1,0:T(8,128)(2,1)S(1)}, u32[]{:S(2)}, u32[]{:S(2)}) async-start(bf16[16,2,32,8,128]{4,3,2,1,0:T(8,128)(2,1)} %shard_map.46), calls=%async_computation.1 | async-start | bytes 4194304 | tf_op jit(solution)/shard_map/all_to_all | solution.py:154
  189.9 3.5 %copy-start.1 = (bf16[4,2,2,2,32,2048]{5,4,3,2,1,0:T(8,128)(2,1)S(1)}, bf16[4,2,2,2,32,2048]{5,4,3,2,1,0:T(8,128)(2,1)}, u32[]{:S(2)}) copy-start(bf16[4,2,2,2,32,2048]{5,4,3,2,1,0:T(8,128)(2,1)} %constant.33) | copy-start | bytes 12582916
  189.9 4.7 %copy-start.2 = (bf16[4,2,2,2,32,2048]{5,4,3,2,1,0:T(8,128)(2,1)S(1)}, bf16[4,2,2,2,32,2048]{5,4,3,2,1,0:T(8,128)(2,1)}, u32[]{:S(2)}) copy-start(bf16[4,2,2,2,32,2048]{5,4,3,2,1,0:T(8,128)(2,1)} %constant.34) | copy-start | bytes 12582916

commit v6 on v5

--- a/solution.py
+++ b/solution.py
@@ -96,7 +96,7 @@
 
 def cross(own_t, next_t, wrap_t, parts, interpret=False):
     two, width, block, segs = own_t.shape
-    step = min(width, 8)
+    step = min(width, 16)
     spec = pl.BlockSpec((two, step, block, segs), lambda i: (0, i, 0, 0))
     return pl.pallas_call(
         cross_kernel,

time: 228 us -> 228 us (level)
  no operation moved by 1% of the time
where the time goes in v6:
time: 228 us
  waiting for transfers between devices  99.7 us (44%)
  Pallas kernels  35.8 us (16%)
  starting transfers between devices  30.9 us (14%)
  matrix products  30.6 us (13%)
  local copies, waits for them, and re-layouts  16.4 us (7%)
  other arithmetic  14 us (6%)
    all_to_all x2, waiting for transfers between devices, body(): own = lax.all_to_all(piece, 'tm', split_axis=0, concat_axis=1, tiled=True)  41.5 us
    pallas_call x2, Pallas kernels, cross(): pl.pallas_call(cross_kernel, grid=(width // step,), in_specs=[spec, spec,...  35.8 us
    ppermute x2, waiting for transfers between devices, body(): next_t = lax.ppermute(own_t, 'chan', inner_route)  27.9 us
    dot_general x2, matrix products, body(): jnp.einsum('hak,hl->akl', gathered, rows, preferred_element_type=jnp.floa...  18 us
    ppermute x2, waiting for transfers between devices, body(): wrap_t = lax.ppermute(own_t, ('chan', 'tm'), wrap_route)  17.9 us
    dot_general x1, matrix products, body(): jnp.einsum('jat,tc->cja', traces, table, preferred_element_type=jnp.float32)  12.5 us
    all_to_all x2, waiting for transfers between devices, body(): lax.all_to_all(stack, 'tm', split_axis=0, concat_axis=0, tiled=True)  12.3 us
    all_to_all x2, starting transfers between devices, body(): own = lax.all_to_all(piece, 'tm', split_axis=0, concat_axis=1, tiled=True)  10.9 us
  transfers between devices with their start and end apart: 8, of which 7 were waited for; matrix products, arithmetic and copies ran while one was open for 11% of the time, Pallas kernels for 16%

profile of v6, /device:TPU:6, one launch (start us, length us, event | category | flops | bytes accessed | tf_op | source)
XLA Modules:
  0.0 227.6 jit_solution(10405325826584487728)
XLA Ops:
  0.0 12.5 %fusion.12 = f32[2048,8,128]{2,0,1:T(8,128)S(1)} fusion(bf16[2048,2048,1]{0,1,2:T(8,128)(2,1)} %constant.38, bf16[8,128,2048]{2,1,0:T(8,128)(2,1)} %param.4), kind=kOutput, calls=%fused_computation.23 | convolution fusion | flops 8589934592 | bytes 20971520 | tf_op jit(solution)/shard_map/jat,tc->cja/dot_general | solution.py:128
  17.7 2.2 fusion.11
  19.8 3.3 %copy.11 = bf16[4,2,2,2,32,8,128]{6,5,4,3,2,1,0:T(8,128)(2,1)S(1)} copy(bf16[4,2,2,2,32,8,128]{6,4,3,2,1,0,5:T(8,128)(2,1)S(1)} %bitcast.47) | data formatting | bytes 4194304 | tf_op jit(solution)/shard_map/reshape;squeeze | solution.py:143
  25.1 6.4 %all-to-all-start.2 = ((bf16[1024,8,128]{2,1,0:T(8,128)(2,1)}), bf16[1024,8,128]{2,1,0:T(8,128)(2,1)S(1)}, u32[]{:S(2)}, u32[]{:S(2)}) async-start(bf16[1024,8,128]{2,1,0:T(8,128)(2,1)} %bitcast.42), calls=%async_computation.2 | async-start | bytes 4194304 | tf_op jit(solution)/shard_map/all_to_all | solution.py:149
  31.5 4.9 %copy.7 = bf16[4,2,2,2,32,8,128]{6,5,4,3,2,1,0:T(8,128)(2,1)S(1)} copy(bf16[4,2,2,2,32,8,128]{6,4,3,2,1,0,5:T(8,128)(2,1)} %bitcast.46) | data formatting | bytes 4194304 | tf_op jit(solution)/shard_map/reshape;squeeze | solution.py:143
  38.3 21.0 %all-to-all-done.2 = bf16[1024,8,128]{2,1,0:T(8,128)(2,1)S(1)} async-done(((bf16[1024,8,128]{2,1,0:T(8,128)(2,1)}), bf16[1024,8,128]{2,1,0:T(8,128)(2,1)S(1)}, u32[]{:S(2)}, u32[]{:S(2)}) %all-to-all-start.2) | async-done | bytes 2097184 | tf_op jit(solution)/shard_map/all_to_all | solution.py:149
  59.3 4.4 %all-to-all-start = ((bf16[1024,8,128]{2,1,0:T(8,128)(2,1)}), bf16[1024,8,128]{2,1,0:T(8,128)(2,1)}, u32[]{:S(2)}, u32[]{:S(2)}) async-start(bf16[1024,8,128]{2,1,0:T(8,128)(2,1)} %bitcast.7), calls=%async_computation | async-start | bytes 4194304 | tf_op jit(solution)/shard_map/all_to_all | solution.py:149
  65.7 4.1 %collective-permute-start.2 = (bf16[2,32,128,128]{3,2,1,0:T(8,128)(2,1)}, bf16[2,32,128,128]{3,2,1,0:T(8,128)(2,1)}, u32[]{:S(2)}, u32[]{:S(2)}) collective-permute-start(bf16[2,32,128,128]{3,2,1,0:T(8,128)(2,1)} %bitcast.18.own_ref), channel_id=1, source_target_pairs={{16,0},{32,16},{48,32},{80,64},{96,80},{112,96},{17,1},{33,17},{49... | collective-permute-start | bytes 6291464 | tf_op jit(solution)/shard_map/ppermute | solution.py:151
  71.0 20.6 %all-to-all-done = bf16[1024,8,128]{2,1,0:T(8,128)(2,1)} async-done(((bf16[1024,8,128]{2,1,0:T(8,128)(2,1)}), bf16[1024,8,128]{2,1,0:T(8,128)(2,1)}, u32[]{:S(2)}, u32[]{:S(2)}) %all-to-all-start) | async-done | bytes 2097184 | tf_op jit(solution)/shard_map/all_to_all | solution.py:149
  91.6 2.2 copy.9
  93.8 4.1 %collective-permute-start = (bf16[2,32,128,128]{3,2,1,0:T(8,128)(2,1)S(1)}, bf16[2,32,128,128]{3,2,1,0:T(8,128)(2,1)}, u32[]{:S(2)}, u32[]{:S(2)}) collective-permute-start(bf16[2,32,128,128]{3,2,1,0:T(8,128)(2,1)S(1)} %bitcast.43), channel_id=1, source_target_pairs={{16,0},{32,16},{48,32},{80,64},{96,80},{112,96},{17,1},{33,17},{49... | collective-permute-start | bytes 6291464 | tf_op jit(solution)/shard_map/ppermute | solution.py:151
  99.2 15.5 %collective-permute-done.2.next_ref = bf16[2,32,128,128]{3,2,1,0:T(8,128)(2,1)} collective-permute-done((bf16[2,32,128,128]{3,2,1,0:T(8,128)(2,1)}, bf16[2,32,128,128]{3,2,1,0:T(8,128)(2,1)}, u32[]{:S(2)}, u32[]{:S(2)}) %collective-permute-start.2) | collective-permute-done | bytes 2097184 | tf_op jit(solution)/shard_map/ppermute | solution.py:151
  114.7 9.0 %collective-permute-done.3.wrap_ref = bf16[2,32,128,128]{3,2,1,0:T(8,128)(2,1)} collective-permute-done((bf16[2,32,128,128]{3,2,1,0:T(8,128)(2,1)}, bf16[2,32,128,128]{3,2,1,0:T(8,128)(2,1)}, u32[]{:S(2)}, u32[]{:S(2)}) %collective-permute-start.3) | collective-permute-done | bytes 2097184 | tf_op jit(solution)/shard_map/ppermute | solution.py:152
  123.8 17.9 %shard_map.47 = bf16[16,2,32,8,128]{4,3,2,1,0:T(8,128)(2,1)} custom-call(bf16[2,32,128,128]{3,2,1,0:T(8,128)(2,1)} %bitcast.18.own_ref, bf16[2,32,128,128]{3,2,1,0:T(8,128)(2,1)} %collective-permute-done.2.next_ref, bf16[2,32,128,128]{3,2,1,0:T(8,128)(2,1)} %collective-permute-done.3.wrap_ref), custom_call_target="tpu_custom_call" | custom-call | tf_op jit(solution)/shard_map/pallas_call | solution.py:101
  141.7 4.7 %all-to-all-start.3 = ((bf16[16,2,32,8,128]{4,3,2,1,0:T(8,128)(2,1)}), bf16[16,2,32,8,128]{4,3,2,1,0:T(8,128)(2,1)}, u32[]{:S(2)}, u32[]{:S(2)}) async-start(bf16[16,2,32,8,128]{4,3,2,1,0:T(8,128)(2,1)} %shard_map.47), calls=%async_computation.3 | async-start | bytes 4194304 | tf_op jit(solution)/shard_map/all_to_all | solution.py:154
  146.4 12.4 %collective-permute-done.next_ref = bf16[2,32,128,128]{3,2,1,0:T(8,128)(2,1)} collective-permute-done((bf16[2,32,128,128]{3,2,1,0:T(8,128)(2,1)S(1)}, bf16[2,32,128,128]{3,2,1,0:T(8,128)(2,1)}, u32[]{:S(2)}, u32[]{:S(2)}) %collective-permute-start) | collective-permute-done | bytes 2097184 | tf_op jit(solution)/shard_map/ppermute | solution.py:151
  158.8 8.9 %collective-permute-done.1.wrap_ref = bf16[2,32,128,128]{3,2,1,0:T(8,128)(2,1)} collective-permute-done((bf16[2,32,128,128]{3,2,1,0:T(8,128)(2,1)S(1)}, bf16[2,32,128,128]{3,2,1,0:T(8,128)(2,1)}, u32[]{:S(2)}, u32[]{:S(2)}) %collective-permute-start.1) | collective-permute-done | bytes 2097184 | tf_op jit(solution)/shard_map/ppermute | solution.py:152
  167.7 17.9 %shard_map.46 = bf16[16,2,32,8,128]{4,3,2,1,0:T(8,128)(2,1)} custom-call(bf16[2,32,128,128]{3,2,1,0:T(8,128)(2,1)} %bitcast.45, bf16[2,32,128,128]{3,2,1,0:T(8,128)(2,1)} %collective-permute-done.next_ref, bf16[2,32,128,128]{3,2,1,0:T(8,128)(2,1)} %collective-permute-done.1.wrap_ref), custom_call_target="tpu_custom_call" | custom-call | tf_op jit(solution)/shard_map/pallas_call | solution.py:101
  185.6 4.6 %all-to-all-start.1 = ((bf16[16,2,32,8,128]{4,3,2,1,0:T(8,128)(2,1)}), bf16[16,2,32,8,128]{4,3,2,1,0:T(8,128)(2,1)S(1)}, u32[]{:S(2)}, u32[]{:S(2)}) async-start(bf16[16,2,32,8,128]{4,3,2,1,0:T(8,128)(2,1)} %shard_map.46), calls=%async_computation.1 | async-start | bytes 4194304 | tf_op jit(solution)/shard_map/all_to_all | solution.py:154
  190.2 2.8 %broadcast_select_fusion = bf16[4,2,2,2,32,2048]{5,4,3,2,1,0:T(8,128)(2,1)S(1)} fusion(bf16[4,2,2,2,32,2048]{5,4,3,2,1,0:T(8,128)(2,1)} %constant.37, bf16[4,2,2,2,32,2048]{5,4,3,2,1,0:T(8,128)(2,1)} %constant.36, pred[]{:T(512)S(6)} %lt.3), kind=kLoop, calls=%fused_computation.13 | loop fusion | flops 2097152 | bytes 12582913 | tf_op jit(solution)/shard_map/jit(_where)/select_n | solution.py:144
  194.9 2.4 %broadcast_select_fusion.1 = bf16[4,2,2,2,32,2048]{5,4,3,2,1,0:T(8,128)(2,1)} fusion(bf16[4,2,2,2,32,2048]{5,4,3,2,1,0:T(8,128)(2,1)S(1)} %copy-done.2, bf16[4,2,2,2,32,2048]{5,4,3,2,1,0:T(8,128)(2,1)S(1)} %copy-done.1, pred[]{:T(512)S(6)} %lt.3), kind=kLoop, calls=%fused_computation.14 | loop fusion | flops 2097152 | bytes 12582913 | tf_op jit(solution)/shard_map/jit(_where)/select_n | solution.py:144
  197.3 8.4 %fusion.6 = f32[8,128,2048]{2,1,0:T(8,128)} fusion(bf16[1024,2048,1]{1,0,2:T(8,128)(2,1)S(1)} %bitcast.48, bf16[1024,8,128]{2,1,0:T(8,128)(2,1)} %bitcast.19), kind=kOutput, calls=%fused_computation.17 | convolution fusion | flops 4294967296 | bytes 14680064 | tf_op jit(solution)/shard_map/hak,hl->akl/dot_general | solution.py:157
  205.7 12.3 %all-to-all-done.1 = bf16[16,2,32,8,128]{4,3,2,1,0:T(8,128)(2,1)S(1)} async-done(((bf16[16,2,32,8,128]{4,3,2,1,0:T(8,128)(2,1)}), bf16[16,2,32,8,128]{4,3,2,1,0:T(8,128)(2,1)S(1)}, u32[]{:S(2)}, u32[]{:S(2)}) %all-to-all-start.1) | async-done | bytes 2097184 | tf_op jit(solution)/shard_map/all_to_all | solution.py:154
  218.0 9.6 %add_convert_fusion = bf16[8,128,2048]{2,1,0:T(8,128)(2,1)} fusion(f32[8,128,2048]{2,1,0:T(8,128)} %fusion.6, bf16[1024,2048,1]{1,0,2:T(8,128)(2,1)} %bitcast.39, bf16[1024,8,128]{2,1,0:T(8,128)(2,1)S(1)} %bitcast.40), kind=kOutput, calls=%fused_computation.3 | convolution fusion | flops 4299161600 | bytes 18874368 | tf_op jit(solution)/shard_map/hak,hl->akl/dot_general | solution.py:157
  (20 shorter events, 15.3 us)
Async XLA Ops:
  14.2 1.1 copy-start.3
  25.1 34.3 %all-to-all-start.2 = ((bf16[1024,8,128]{2,1,0:T(8,128)(2,1)}), bf16[1024,8,128]{2,1,0:T(8,128)(2,1)S(1)}, u32[]{:S(2)}, u32[]{:S(2)}) async-start(bf16[1024,8,128]{2,1,0:T(8,128)(2,1)} %bitcast.42), calls=%async_computation.2 | async-start | bytes 4194304 | tf_op jit(solution)/shard_map/all_to_all | solution.py:149
  59.3 32.3 %all-to-all-start = ((bf16[1024,8,128]{2,1,0:T(8,128)(2,1)}), bf16[1024,8,128]{2,1,0:T(8,128)(2,1)}, u32[]{:S(2)}, u32[]{:S(2)}) async-start(bf16[1024,8,128]{2,1,0:T(8,128)(2,1)} %bitcast.7), calls=%async_computation | async-start | bytes 4194304 | tf_op jit(solution)/shard_map/all_to_all | solution.py:149
  65.7 49.1 %collective-permute-start.2 = (bf16[2,32,128,128]{3,2,1,0:T(8,128)(2,1)}, bf16[2,32,128,128]{3,2,1,0:T(8,128)(2,1)}, u32[]{:S(2)}, u32[]{:S(2)}) collective-permute-start(bf16[2,32,128,128]{3,2,1,0:T(8,128)(2,1)} %bitcast.18.own_ref), channel_id=1, source_target_pairs={{16,0},{32,16},{48,32},{80,64},{96,80},{112,96},{17,1},{33,17},{49... | collective-permute-start | bytes 6291464 | tf_op jit(solution)/shard_map/ppermute | solution.py:151
  69.7 54.0 %collective-permute-start.3 = (bf16[2,32,128,128]{3,2,1,0:T(8,128)(2,1)}, bf16[2,32,128,128]{3,2,1,0:T(8,128)(2,1)}, u32[]{:S(2)}, u32[]{:S(2)}) collective-permute-start(bf16[2,32,128,128]{3,2,1,0:T(8,128)(2,1)} %bitcast.18.own_ref), channel_id=1, source_target_pairs={{64,50},{65,51},{66,48},{67,49},{68,54},{69,55},{70,52},{71,53},{7... | collective-permute-start | bytes 6291464 | tf_op jit(solution)/shard_map/ppermute | solution.py:152
  93.8 47.9 %copy-start = (bf16[64,16,8,128]{3,2,1,0:T(8,128)(2,1)}, bf16[64,16,8,128]{3,2,1,0:T(8,128)(2,1)S(1)}, u32[]{:S(2)}) copy-start(bf16[64,16,8,128]{3,2,1,0:T(8,128)(2,1)S(1)} %copy.9) | copy-start | bytes 6291460
  93.8 65.0 %collective-permute-start = (bf16[2,32,128,128]{3,2,1,0:T(8,128)(2,1)S(1)}, bf16[2,32,128,128]{3,2,1,0:T(8,128)(2,1)}, u32[]{:S(2)}, u32[]{:S(2)}) collective-permute-start(bf16[2,32,128,128]{3,2,1,0:T(8,128)(2,1)S(1)} %bitcast.43), channel_id=1, source_target_pairs={{16,0},{32,16},{48,32},{80,64},{96,80},{112,96},{17,1},{33,17},{49... | collective-permute-start | bytes 6291464 | tf_op jit(solution)/shard_map/ppermute | solution.py:151
  97.9 69.8 %collective-permute-start.1 = (bf16[2,32,128,128]{3,2,1,0:T(8,128)(2,1)S(1)}, bf16[2,32,128,128]{3,2,1,0:T(8,128)(2,1)}, u32[]{:S(2)}, u32[]{:S(2)}) collective-permute-start(bf16[2,32,128,128]{3,2,1,0:T(8,128)(2,1)S(1)} %bitcast.44), channel_id=1, source_target_pairs={{64,50},{65,51},{66,48},{67,49},{68,54},{69,55},{70,52},{71,53},{7... | collective-permute-start | bytes 6291464 | tf_op jit(solution)/shard_map/ppermute | solution.py:152
  141.7 43.9 %all-to-all-start.3 = ((bf16[16,2,32,8,128]{4,3,2,1,0:T(8,128)(2,1)}), bf16[16,2,32,8,128]{4,3,2,1,0:T(8,128)(2,1)}, u32[]{:S(2)}, u32[]{:S(2)}) async-start(bf16[16,2,32,8,128]{4,3,2,1,0:T(8,128)(2,1)} %shard_map.47), calls=%async_computation.3 | async-start | bytes 4194304 | tf_op jit(solution)/shard_map/all_to_all | solution.py:154
  185.6 32.4 %all-to-all-start.1 = ((bf16[16,2,32,8,128]{4,3,2,1,0:T(8,128)(2,1)}), bf16[16,2,32,8,128]{4,3,2,1,0:T(8,128)(2,1)S(1)}, u32[]{:S(2)}, u32[]{:S(2)}) async-start(bf16[16,2,32,8,128]{4,3,2,1,0:T(8,128)(2,1)} %shard_map.46), calls=%async_computation.1 | async-start | bytes 4194304 | tf_op jit(solution)/shard_map/all_to_all | solution.py:154
  190.2 3.5 %copy-start.1 = (bf16[4,2,2,2,32,2048]{5,4,3,2,1,0:T(8,128)(2,1)S(1)}, bf16[4,2,2,2,32,2048]{5,4,3,2,1,0:T(8,128)(2,1)}, u32[]{:S(2)}) copy-start(bf16[4,2,2,2,32,2048]{5,4,3,2,1,0:T(8,128)(2,1)} %constant.33) | copy-start | bytes 12582916
  190.2 4.7 %copy-start.2 = (bf16[4,2,2,2,32,2048]{5,4,3,2,1,0:T(8,128)(2,1)S(1)}, bf16[4,2,2,2,32,2048]{5,4,3,2,1,0:T(8,128)(2,1)}, u32[]{:S(2)}) copy-start(bf16[4,2,2,2,32,2048]{5,4,3,2,1,0:T(8,128)(2,1)} %constant.34) | copy-start | bytes 12582916
